TPU v7x, 512 devices: a whole 4x4x16 slice. The times are simulated.
512 devices in a mesh: row: 16 (over x, y), col: 32 (over z, core).
Axes of the slice: x: 4, y: 4, z: 16, core: 2. Of those that a mesh axis runs over, the one named last changes fastest.
Arguments:
- hidden: bfloat16 [2560, 7168], P('col', 'row'), may hold values from -6 to 6
- ln_gain: bfloat16 [7168], P('row'), may hold values from 0.099609375 to 1.8984375
- ln_shift: bfloat16 [7168], P('row'), may hold values from -3 to 3
- qkv_weight: bfloat16 [7168, 12288], P('row', 'col'), may hold values from -0.0625 to 0.0625
- qkv_bias: bfloat16 [12288], P('col'), may hold values from -5.351432 to 5.351432
- out_weight: bfloat16 [4096, 7168], P('row', 'col'), may hold values from -0.09375 to 0.09375
- out_bias: bfloat16 [7168], P('col'), may hold values from -3 to 3
- down_qkv: bfloat16 [64, 7168, 16], P(None, 'row'), may hold values from -0.0625 to 0.0625
- up_qkv: bfloat16 [64, 16, 12288], P(None, None, 'col'), may hold values from -1.5 to 1.5
- down_out: bfloat16 [64, 16, 4096], P(None, None, 'col'), may hold values from -0.09375 to 0.09375
- up_out: bfloat16 [64, 16, 7168], P(None, None, 'col'), may hold values from -1.5 to 1.5
- prompt_lens: int32 [16], replicated, may hold values from 1 to 80, as said below
- suffix_lens: int32 [16, 16], replicated, may hold values from 1 to 5, as said below
- group_sizes: int32 [16], replicated, may hold values from 8 to 16, as said below
- group_adapter_choice: int32 [16], replicated, may hold values from 0 to 15
- chosen: int32 [16], replicated, may hold values from 0 to 63, as said below
Outputs:
- attn_out: bfloat16 [2560, 7168], P('row', 'col')
Inputs may be any that keep to these rules, and one draw needn't show every extreme that they name: `prompt_lens`: one group, drawn from the seed, has a prompt of exactly 80 tokens, 16 requests and every suffix 5 long, so it fills all 160 slots. `suffix_lens`: entries past a group's number of requests are not used. `group_sizes`: A group's prompt and its live suffixes take at most 160 slots. `chosen`: 16 different bank indices.
All inputs are finite; a program needn't handle non-finite values.
Results may differ from a plain program's by a relative error of at most 0.012.
The roundings to bfloat16 on the way count: a program that leaves them out, or rounds other values in their place, can miss the bound.
Values may be sent and summed in bfloat16 or wider, within the bound.
No kernel may reach another device: no remote copies, remote signals or barrier semaphores. Data moves between devices by JAX's collectives and lax.ppermute only.
A program may use at most 64 MiB of HBM per device.

v0:
```python
import jax
import jax.numpy as jnp
from jax import lax
from jax.sharding import PartitionSpec as P

HEAD_SIZE = 128
GCAP = 160
WIN = 53


def broadcast(x, axis, root):
    mine = lax.axis_index(axis) == root
    return lax.psum(jnp.where(mine, x, jnp.zeros_like(x)), axis)


def group_layout(prompt, count, suffix):
    offsets = jnp.arange(GCAP, dtype=jnp.int32)
    chosen_adapter_index = jnp.arange(suffix.shape[0], dtype=jnp.int32)
    live_lens = jnp.where(chosen_adapter_index < count, suffix, 0)
    end_at = prompt + jnp.cumsum(live_lens)
    group_start_rows = end_at - live_lens
    request = jnp.sum((offsets[:, None] >= end_at[None, :]).astype(jnp.int32), axis=1)
    in_prompt = offsets < prompt
    live_rows = in_prompt | (request < count)
    group_begin_row = jnp.sum(
        jnp.where(chosen_adapter_index[None, :] == request[:, None], group_start_rows[None, :], 0),
        axis=1,
    )
    position = jnp.where(in_prompt, offsets, prompt + offsets - group_begin_row)
    request_of = jnp.where(in_prompt, -1, request)
    return (live_rows, request_of, position)


def key_mask(live_rows, request_of, position):
    shared = (request_of[None, :] == -1) | (request_of[None, :] == request_of[:, None])
    causal = position[None, :] <= position[:, None]
    within = (position[:, None] - position[None, :] < WIN) | (position[None, :] == 0)
    allowed = live_rows[:, None] & live_rows[None, :] & shared & causal & within
    first_key = jnp.arange(GCAP)[None, :] == 0
    return jnp.where(live_rows[:, None], allowed, first_key)


def attention(queries, key_rows, value_rows, allowed):
    scores = jnp.einsum("qhe,khe->hqk", queries, key_rows, preferred_element_type=jnp.float32)
    scores = jnp.where(allowed[None], scores, -1e30)
    highest = jnp.max(scores, axis=2, keepdims=True)
    weights = jnp.where(allowed[None], jnp.exp(scores - highest), 0.0)
    probs = (weights / jnp.sum(weights, axis=2, keepdims=True)).astype(jnp.bfloat16)
    mixed_rows = jnp.einsum("hqk,khe->qhe", probs, value_rows, preferred_element_type=jnp.float32)
    return mixed_rows.astype(jnp.bfloat16).reshape(queries.shape[0], -1)


def local(
    hidden,
    ln_gain,
    ln_shift,
    qkv_weight,
    qkv_bias,
    out_weight,
    out_bias,
    down_qkv,
    up_qkv,
    down_out,
    up_out,
    prompt_lens,
    suffix_lens,
    group_sizes,
    group_adapter_choice,
    chosen,
):
    row_index = lax.axis_index("row")
    row_count = lax.axis_size("row")
    adapters = chosen[group_adapter_choice]
    own_adapter = adapters[row_index]
    low_rank = down_qkv.shape[2]
    features, gain_full, shift_full = (
        lax.all_gather(hidden, "row", axis=1, tiled=True),
        lax.all_gather(ln_gain, "row", axis=0, tiled=True),
        lax.all_gather(ln_shift, "row", axis=0, tiled=True),
    )
    widened = features.astype(jnp.float32)
    average = jnp.mean(widened, axis=1, keepdims=True)
    centred = widened - average
    spread = jnp.mean(centred * centred, axis=1, keepdims=True)
    normed = (
        centred * lax.rsqrt(spread + 1e-05) * gain_full.astype(jnp.float32)
        + shift_full.astype(jnp.float32)
    ).astype(jnp.bfloat16)
    per_group = lax.axis_size("col") // row_count
    received = []
    for offset in range(per_group):
        received.append(broadcast(normed, "col", row_index * per_group + offset))
    group_rows = jnp.concatenate(received, axis=0)
    lowered = jnp.transpose(down_qkv[adapters], (1, 0, 2)).reshape(
        down_qkv.shape[1], row_count * low_rank
    )
    sliced = group_rows
    own_down = lax.dynamic_slice_in_dim(
        lax.all_gather(lowered, "row", axis=0, tiled=True), row_index * low_rank, low_rank, 1
    )
    projected = jnp.dot(
        sliced,
        lax.all_gather(qkv_weight, "row", axis=0, tiled=True),
        preferred_element_type=jnp.float32,
    )
    reduced = jnp.dot(sliced, own_down, preferred_element_type=jnp.float32)
    projected = (
        projected
        + qkv_bias.astype(jnp.float32)
        + jnp.dot(
            reduced.astype(jnp.bfloat16), up_qkv[own_adapter], preferred_element_type=jnp.float32
        )
    )
    heads_here = projected.shape[1] // (3 * HEAD_SIZE)
    shaped = projected.reshape(GCAP, heads_here, 3, HEAD_SIZE)
    queries = (shaped[:, :, 0] * HEAD_SIZE ** (-0.5)).astype(jnp.bfloat16)
    key_rows = shaped[:, :, 1].astype(jnp.bfloat16)
    value_rows = shaped[:, :, 2].astype(jnp.bfloat16)
    live_rows, request_of, position = group_layout(
        prompt_lens[row_index], group_sizes[row_index], suffix_lens[row_index]
    )
    mixed_rows = attention(queries, key_rows, value_rows, key_mask(live_rows, request_of, position))
    down_here = down_out[own_adapter]
    all_heads, down_full = (
        lax.all_gather(mixed_rows, "col", axis=1, tiled=True),
        lax.all_gather(down_here, "col", axis=1, tiled=True),
    )
    reduced_out = lax.dot_general(
        all_heads, down_full, (((1,), (1,)), ((), ())), preferred_element_type=jnp.float32
    ).astype(jnp.bfloat16)
    sliced = all_heads
    combined = jnp.dot(
        sliced,
        lax.all_gather(out_weight, "row", axis=0, tiled=True),
        preferred_element_type=jnp.float32,
    )
    result = (
        combined
        + out_bias.astype(jnp.float32)
        + jnp.dot(reduced_out, up_out[own_adapter], preferred_element_type=jnp.float32)
    )
    return (result * live_rows[:, None].astype(jnp.float32)).astype(jnp.bfloat16)


def solution(mesh):
    in_specs = (
        P("col", "row"),
        P("row"),
        P("row"),
        P("row", "col"),
        P("col"),
        P("row", "col"),
        P("col"),
        P(None, "row", None),
        P(None, None, "col"),
        P(None, None, "col"),
        P(None, None, "col"),
        P(),
        P(),
        P(),
        P(),
        P(),
    )
    out_specs = P("row", "col")
    return jax.shard_map(local, mesh=mesh, in_specs=in_specs, out_specs=out_specs, check_vma=False)
```

profile of v0, /device:TPU:1, one launch (start us, length us, event | category | flops | bytes accessed | tf_op | source)
XLA Modules:
  0.0 602.8 jit_solution(5477577475409524125)
XLA Ops:
  6.5 0.7 all-gather.17.cloned.1.call-update
  7.3 1.3 dynamic-slice
  9.3 0.9 dynamic-update-slice
  10.1 0.9 dynamic-update-slice.1
  11.0 61.8 %all-reduce.3 = (bf16[7168]{0:T(1024)(128)(2,1)S(1)}, bf16[7168]{0:T(1024)(128)(2,1)S(1)}) all-reduce(bf16[7168]{0:T(1024)(128)(2,1)S(1)} %dynamic-update-slice, bf16[7168]{0:T(1024)(128)(2,1)S(1)} %dynamic-update-slice.1), channel_id=1, replica_groups=mesh['row'=16,'col'=32] {'row'}, use_global_device_ids=true, to_apply=%add | all-reduce | flops 14336 | bytes 57344
  72.9 3.6 copy.26
  76.5 2.4 reshape.225
  78.9 1.6 convert_reduce_fusion
  80.5 0.4 multiply_reduce_fusion
  80.9 1.6 broadcast_select_fusion
  82.5 1.2 broadcast_select_fusion.1
  83.8 0.7 all-gather.9.cloned.1.call-update
  84.5 0.7 gather_fusion
  85.3 0.6 gather_fusion.1
  85.8 0.8 copy.27
  86.8 0.6 dynamic_slice.25
  88.7 0.6 dynamic_slice.28
  89.3 1.3 compare_select_fusion.3
  90.6 0.1 copy.28
  90.7 0.6 dynamic_slice.27
  92.0 0.7 add_reduce_fusion
  92.8 0.1 convert_reduce_fusion.1
  92.9 1.3 fusion.54
  94.2 0.1 select_reduce_fusion
  94.3 0.6 broadcast_compare_fusion
  94.9 1.3 fusion.57
  96.2 216.5 %all-reduce.6.cloned.1.call-done = (bf16[80,7168]{1,0:T(8,128)(2,1)}, bf16[80,7168]{1,0:T(8,128)(2,1)}) async-done(((bf16[80,7168]{1,0:T(8,128)(2,1)}, bf16[80,7168]{1,0:T(8,128)(2,1)}), (bf16[80,7168]{1,0:T(8,128)(2,1)}, bf16[80,7168]{1,0:T(8,128)(2,1)})) %all-reduce.6.cloned.1.call-update) | async-done | bytes 2293776 | tf_op jit(solution)/shard_map/psum | solution.py:13
  312.7 1.4 constant_dynamic-update-slice_fusion.1
  314.2 0.2 copy-done.2
  314.3 0.1 constant_dynamic-update-slice_fusion
  314.4 75.2 %all-gather.9.cloned.1.call-done = bf16[7168,384]{1,0:T(8,128)(2,1)} async-done(((bf16[448,384]{1,0:T(8,128)(2,1)}), bf16[7168,384]{1,0:T(8,128)(2,1)}) %all-gather.9.cloned.1.call-update) | async-done | bytes 5505040 | tf_op jit(solution)/shard_map/all_gather | solution.py:103
  389.6 4.6 convolution_add_fusion.1
  394.2 62.6 %all-gather.11.cloned.1.call-done = bf16[7168,256]{1,0:T(8,128)(2,1)} async-done(((bf16[448,256]{1,0:T(8,128)(2,1)}), bf16[7168,256]{1,0:T(8,128)(2,1)}) %all-gather.11.cloned.1.call-update) | async-done | bytes 3670032 | tf_op jit(solution)/shard_map/all_gather | solution.py:99
  456.9 4.1 convolution_add_fusion
  461.0 1.1 reshape.192
  462.0 0.1 convert.4
  462.1 0.1 fusion.37
  462.2 0.2 fusion.60
  462.4 0.2 fusion.61
  462.6 0.2 fusion.36
  462.8 1.0 fusion.19
  463.9 0.5 all-gather.13.cloned.1.call-update
  464.4 0.7 constant_dynamic-slice_fusion
  465.1 32.3 %all-gather.1 = bf16[1,16,4096]{2,1,0:T(8,128)(2,1)S(1)} all-gather(bf16[1,16,128]{2,1,0:T(8,128)(2,1)S(1)} %constant_dynamic-slice_fusion), channel_id=3, replica_groups=mesh['row'=16,'col'=32] {'col'}, dimensions={2}, use_global_device_ids=true | all-gather | bytes 135168 | tf_op jit(solution)/shard_map/all_gather | solution.py:126
  497.5 37.3 %all-gather.15.cloned.1.call-done = bf16[160,1,4096]{2,0,1:T(8,128)(2,1)} async-done(((bf16[160,1,128]{2,0,1:T(8,128)(2,1)}), bf16[160,1,4096]{2,0,1:T(8,128)(2,1)}) %all-gather.15.cloned.1.call-update) | async-done | bytes 1310736 | tf_op jit(solution)/shard_map/all_gather | solution.py:125
  534.7 2.0 fusion.27
  536.8 55.9 %all-gather.13.cloned.1.call-done = bf16[4096,224]{0,1:T(8,128)(2,1)} async-done(((bf16[256,224]{0,1:T(8,128)(2,1)}), bf16[4096,224]{0,1:T(8,128)(2,1)}) %all-gather.13.cloned.1.call-update) | async-done | bytes 1835024 | tf_op jit(solution)/shard_map/all_gather | solution.py:134
  592.6 3.3 fusion.16
  (39 shorter events, 0.4 us)
Async XLA Ops:
  6.5 78.7 %copy-start = (bf16[64,448,16]{1,2,0:T(8,128)(2,1)S(1)}, bf16[64,448,16]{1,2,0:T(8,128)(2,1)}, u32[]{:S(2)}) copy-start(bf16[64,448,16]{1,2,0:T(8,128)(2,1)} %param.23) | copy-start | bytes 2752516
  6.5 66.3 %all-gather.17.cloned.1.call-start = ((), (), s32[]{:S(2)}) async-start(), calls=%async_computation.4 | async-start | bytes 1392640 | tf_op jit(solution)/shard_map/all_gather | solution.py:77
  7.3 305.5 %all-reduce.6.cloned.1.call-start = ((), (), s32[]{:S(2)}) async-start(), calls=%async_computation.5 | async-start | bytes 4587520 | tf_op jit(solution)/shard_map/psum | solution.py:13
  82.5 2.0 copy-start.4
  82.5 2.0 copy-start.1
  83.7 305.9 %all-gather.9.cloned.1.call-start = ((), (), s32[]{:S(2)}) async-start(), calls=%async_computation | async-start | bytes 5849088 | tf_op jit(solution)/shard_map/all_gather | solution.py:103
  84.4 372.4 %all-gather.11.cloned.1.call-start = ((), (), s32[]{:S(2)}) async-start(), calls=%async_computation.1 | async-start | bytes 3899392 | tf_op jit(solution)/shard_map/all_gather | solution.py:99
  85.2 1.5 copy-start.3
  85.2 3.4 copy-start.5
  85.2 5.5 copy-start.6
  86.7 448.0 %all-gather.15.cloned.1.call-start = ((), (), s32[]{:S(2)}) async-start(), calls=%async_computation.3 | async-start | bytes 1351680 | tf_op jit(solution)/shard_map/all_gather | solution.py:125
  312.7 1.6 copy-start.2
  461.0 3.4 copy-start.7
  463.8 128.8 %all-gather.13.cloned.1.call-start = ((), (), s32[]{:S(2)}) async-start(), calls=%async_computation.2 | async-start | bytes 1949696 | tf_op jit(solution)/shard_map/all_gather | solution.py:134
Sparse Core Ops, SparseCore 0:
  10.4 61.9 all-gather.16
  83.8 228.8 all-reduce.5
  315.8 73.7 all-gather.8
  392.5 64.3 all-gather.10
  464.0 70.7 all-gather.14
  537.6 54.9 all-gather.12
where the time goes:
time: 604 us; the launch traced here: 603 us
  waiting for transfers between devices  449 us (74%)
  blocking collectives  94.2 us (16%)
  local copies, waits for them, and re-layouts  16.6 us (3%)
  between operations  16.3 us (3%)
  matrix products  15.3 us (3%)
  other arithmetic  10.7 us (2%)
    psum x1, waiting for transfers between devices, broadcast(): return lax.psum(jnp.where(mine, x, jnp.zeros_like(x)), axis)  217 us
    all_gather x1, waiting for transfers between devices, local(): lax.all_gather(qkv_weight, 'row', axis=0, tiled=True)  75.2 us
    all_gather x1, waiting for transfers between devices, local(): lax.all_gather(lowered, 'row', axis=0, tiled=True)  62.6 us
    unnamed x1, blocking collectives  61.8 us
    all_gather x1, waiting for transfers between devices, local(): lax.all_gather(out_weight, 'row', axis=0, tiled=True)  55.9 us
    all_gather x1, waiting for transfers between devices, local(): lax.all_gather(mixed_rows, 'col', axis=1, tiled=True)  37.3 us
    all_gather x1, blocking collectives, local(): lax.all_gather(down_here, 'col', axis=1, tiled=True)  32.3 us
  transfers between devices with their start and end apart: 6, of which 5 were waited for; matrix products, arithmetic and copies ran while one was open for 4% of the time, Pallas kernels for 0%

commit v1 on v0

--- a/solution.py
+++ b/solution.py
@@ -50,6 +50,15 @@
     return mixed_rows.astype(jnp.bfloat16).reshape(queries.shape[0], -1)
 
 
+def rolled_blocks(x, blocks, shift):
+    rows = x.shape[0]
+    width = x.shape[1] // blocks
+    reversed_blocks = x.reshape(rows, blocks, width)[:, ::-1, :]
+    doubled = jnp.concatenate([reversed_blocks, reversed_blocks], axis=1)
+    picked = lax.dynamic_slice_in_dim(doubled, blocks - 1 - shift, blocks, axis=1)
+    return picked.reshape(rows, blocks * width)
+
+
 def local(
     hidden,
     ln_gain,
@@ -69,15 +78,52 @@
     chosen,
 ):
     row_index = lax.axis_index("row")
+    col_index = lax.axis_index("col")
     row_count = lax.axis_size("row")
+    col_count = lax.axis_size("col")
     adapters = chosen[group_adapter_choice]
     own_adapter = adapters[row_index]
-    low_rank = down_qkv.shape[2]
-    features, gain_full, shift_full = (
-        lax.all_gather(hidden, "row", axis=1, tiled=True),
-        lax.all_gather(ln_gain, "row", axis=0, tiled=True),
-        lax.all_gather(ln_shift, "row", axis=0, tiled=True),
+    tokens_here, features_here = hidden.shape
+    chunk = features_here // 2
+
+    blocks_a = []
+    blocks_b = []
+    for shift in range(row_count):
+        target_adapter = adapters[(row_index + shift) % row_count]
+        payload = (
+            jnp.concatenate([qkv_weight, down_qkv[target_adapter]], axis=1),
+            out_weight,
+        )
+        if shift:
+            payload = lax.ppermute(
+                payload, "row", [(i, (i + shift) % row_count) for i in range(row_count)]
+            )
+        blocks_a.append(payload[0])
+        blocks_b.append(payload[1])
+    weight_a = jnp.concatenate(blocks_a, axis=0)
+    weight_b = jnp.concatenate(blocks_b, axis=0)
+
+    payload = jnp.concatenate([hidden, ln_gain[None], ln_shift[None]], axis=0)
+    parity = col_index % 2
+    halves = []
+    for turn in range(2):
+        pairs = [
+            (rp * col_count + cp, (cp // 2) * col_count + 2 * rp + (turn ^ (cp % 2)))
+            for rp in range(row_count)
+            for cp in range(col_count)
+        ]
+        sent = lax.dynamic_slice_in_dim(payload, (turn ^ parity) * chunk, chunk, axis=1)
+        halves.append(lax.ppermute(sent, ("row", "col"), pairs))
+    first = jnp.where(parity == 0, halves[0], halves[1])
+    second = jnp.where(parity == 0, halves[1], halves[0])
+    mine = jnp.stack([first, second])
+    gathered = lax.all_gather(mine, "col", axis=0, tiled=False)
+    features = jnp.transpose(gathered[:, :, :tokens_here, :], (1, 2, 0, 3)).reshape(
+        2 * tokens_here, col_count * chunk
     )
+    gain_full = gathered[:, 0, tokens_here, :].reshape(-1)
+    shift_full = gathered[:, 0, tokens_here + 1, :].reshape(-1)
+
     widened = features.astype(jnp.float32)
     average = jnp.mean(widened, axis=1, keepdims=True)
     centred = widened - average
@@ -86,26 +132,15 @@
         centred * lax.rsqrt(spread + 1e-05) * gain_full.astype(jnp.float32)
         + shift_full.astype(jnp.float32)
     ).astype(jnp.bfloat16)
-    per_group = lax.axis_size("col") // row_count
-    received = []
-    for offset in range(per_group):
-        received.append(broadcast(normed, "col", row_index * per_group + offset))
-    group_rows = jnp.concatenate(received, axis=0)
-    lowered = jnp.transpose(down_qkv[adapters], (1, 0, 2)).reshape(
-        down_qkv.shape[1], row_count * low_rank
+
+    low_rank = down_qkv.shape[2]
+    head_width = qkv_weight.shape[1]
+    projected_all = jnp.dot(
+        rolled_blocks(normed, row_count, row_index), weight_a, preferred_element_type=jnp.float32
     )
-    sliced = group_rows
-    own_down = lax.dynamic_slice_in_dim(
-        lax.all_gather(lowered, "row", axis=0, tiled=True), row_index * low_rank, low_rank, 1
-    )
-    projected = jnp.dot(
-        sliced,
-        lax.all_gather(qkv_weight, "row", axis=0, tiled=True),
-        preferred_element_type=jnp.float32,
-    )
-    reduced = jnp.dot(sliced, own_down, preferred_element_type=jnp.float32)
+    reduced = projected_all[:, head_width:]
     projected = (
-        projected
+        projected_all[:, :head_width]
         + qkv_bias.astype(jnp.float32)
         + jnp.dot(
             reduced.astype(jnp.bfloat16), up_qkv[own_adapter], preferred_element_type=jnp.float32
@@ -121,18 +156,16 @@
     )
     mixed_rows = attention(queries, key_rows, value_rows, key_mask(live_rows, request_of, position))
     down_here = down_out[own_adapter]
-    all_heads, down_full = (
-        lax.all_gather(mixed_rows, "col", axis=1, tiled=True),
-        lax.all_gather(down_here, "col", axis=1, tiled=True),
+    both = lax.all_gather(
+        jnp.concatenate([mixed_rows, down_here], axis=0), "col", axis=0, tiled=False
     )
+    all_heads = jnp.transpose(both[:, :GCAP], (1, 0, 2)).reshape(GCAP, -1)
+    down_full = jnp.transpose(both[:, GCAP:], (1, 0, 2)).reshape(low_rank, -1)
     reduced_out = lax.dot_general(
         all_heads, down_full, (((1,), (1,)), ((), ())), preferred_element_type=jnp.float32
     ).astype(jnp.bfloat16)
-    sliced = all_heads
     combined = jnp.dot(
-        sliced,
-        lax.all_gather(out_weight, "row", axis=0, tiled=True),
-        preferred_element_type=jnp.float32,
+        rolled_blocks(all_heads, row_count, row_index), weight_b, preferred_element_type=jnp.float32
     )
     result = (
         combined

time: 604 us -> 386 us (0.64)
  waiting for transfers between devices: 449 us -> 50.5 us
  starting transfers between devices: 0.2 us -> 178 us
  blocking collectives: 94.2 us -> 0 us
  local copies, waits for them, and re-layouts: 16.6 us -> 64.2 us
  between operations: 16.3 us -> 45.8 us
  other arithmetic: 10.7 us -> 34.7 us
    all_gather x5 -> x2, waiting for transfers between devices: 231 us -> 14.3 us  [the longest x1 14.3 us: local(): lax.all_gather(jnp.concatenate([mixed_rows, down_here], axis=0), 'col', a...]
    psum x1 -> x0, waiting for transfers between devices: 217 us -> none  [broadcast(): return lax.psum(jnp.where(mine, x, jnp.zeros_like(x)), axis)]
    ppermute x0 -> x32, starting transfers between devices: none -> 178 us  [the longest x30 169 us: local(): lax.ppermute(payload, 'row', [(i, (i + shift) % row_count) for i in range...]
    unnamed x1 -> x0, blocking collectives: 61.8 us -> none
    ppermute x0 -> x32, waiting for transfers between devices: none -> 36.1 us  [the longest x30 35.3 us: local(): lax.ppermute(payload, 'row', [(i, (i + shift) % row_count) for i in range...]
    all_gather x1 -> x0, blocking collectives: 32.3 us -> none  [local(): lax.all_gather(down_here, 'col', axis=1, tiled=True)]
    unnamed x22 -> x66, local copies, waits for them, and re-layouts: 4.67 us -> 22.1 us
    concatenate x0 -> x6, other arithmetic: none -> 13 us  [the longest x2 6.83 us: rolled_blocks(): doubled = jnp.concatenate([reversed_blocks, reversed_blocks], axis=1)]
  transfers between devices with their start and end apart: 6 -> 34, of which waited for: 5 -> 6; matrix products, arithmetic and copies ran while one was open for 4% -> 13% of each run, Pallas kernels for 0% -> 0%
where the time goes in v1:
time: 386 us; the launch traced here: 383 us
  starting transfers between devices  178 us (46%)
  local copies, waits for them, and re-layouts  64.2 us (17%)
  waiting for transfers between devices  50.5 us (13%)
  between operations  45.8 us (12%)
  other arithmetic  34.7 us (9%)
  matrix products  10.2 us (3%)
    ppermute x30, starting transfers between devices, local(): lax.ppermute(payload, 'row', [(i, (i + shift) % row_count) for i in range...  169 us
    ppermute x30, waiting for transfers between devices, local(): lax.ppermute(payload, 'row', [(i, (i + shift) % row_count) for i in range...  35.3 us
    unnamed x66, local copies, waits for them, and re-layouts  22.1 us
    all_gather x1, waiting for transfers between devices, local(): lax.all_gather(jnp.concatenate([mixed_rows, down_here], axis=0), 'col', a...  14.3 us
    squeeze x17, local copies, waits for them, and re-layouts, local(): down_qkv[target_adapter]  11.9 us
    ppermute x2, starting transfers between devices, local(): halves.append(lax.ppermute(sent, ('row', 'col'), pairs))  9.41 us
  transfers between devices with their start and end apart: 34, of which 6 were waited for; matrix products, arithmetic and copies ran while one was open for 13% of the time, Pallas kernels for 0%

profile of v1, /device:TPU:1, one launch (start us, length us, event | category | flops | bytes accessed | tf_op | source)
XLA Modules:
  0.0 383.4 jit_solution(1686871920053889677)
XLA Ops:
  9.7 8.7 %collective-permute-start.1 = (bf16[82,224]{1,0:T(8,128)(2,1)S(1)}, bf16[82,224]{1,0:T(8,128)(2,1)S(1)}, u32[]{:S(2)}, u32[]{:S(2)}) collective-permute-start(bf16[82,224]{1,0:T(8,128)(2,1)S(1)} %get-tuple-element.50), channel_id=1, source_target_pairs={{0,1},{1,0},{2,33},{3,32},{4,65},{5,64},{6,97},{7,96},{8,129},{9,1... | collective-permute-start | bytes 110216 | tf_op jit(solution)/shard_map/ppermute | solution.py:116
  55.4 2.2 pad_maximum_fusion
  57.6 6.7 %collective-permute-start.2 = (bf16[448,400]{1,0:T(8,128)(2,1)}, bf16[448,400]{1,0:T(8,128)(2,1)S(1)}, u32[]{:S(2)}, u32[]{:S(2)}) collective-permute-start(bf16[448,400]{1,0:T(8,128)(2,1)} %get-tuple-element.30), channel_id=1, source_target_pairs={{0,32},{32,64},{64,96},{96,128},{128,160},{160,192},{192,224},{224... | collective-permute-start | bytes 1075208 | tf_op jit(solution)/shard_map/ppermute | solution.py:98
  64.4 8.1 %collective-permute-start.3 = (bf16[448,400]{1,0:T(8,128)(2,1)}, bf16[448,400]{1,0:T(8,128)(2,1)S(1)}, u32[]{:S(2)}, u32[]{:S(2)}) collective-permute-start(bf16[448,400]{1,0:T(8,128)(2,1)} %get-tuple-element.31), channel_id=1, source_target_pairs={{0,64},{32,96},{64,128},{96,160},{128,192},{160,224},{192,256},{22... | collective-permute-start | bytes 1075208 | tf_op jit(solution)/shard_map/ppermute | solution.py:98
  72.5 13.5 %collective-permute-start.4 = (bf16[448,400]{1,0:T(8,128)(2,1)}, bf16[448,400]{1,0:T(8,128)(2,1)S(1)}, u32[]{:S(2)}, u32[]{:S(2)}) collective-permute-start(bf16[448,400]{1,0:T(8,128)(2,1)} %get-tuple-element.32), channel_id=1, source_target_pairs={{0,96},{32,128},{64,160},{96,192},{128,224},{160,256},{192,288},{2... | collective-permute-start | bytes 1075208 | tf_op jit(solution)/shard_map/ppermute | solution.py:98
  86.0 10.8 %collective-permute-start.5 = (bf16[448,400]{1,0:T(8,128)(2,1)}, bf16[448,400]{1,0:T(8,128)(2,1)S(1)}, u32[]{:S(2)}, u32[]{:S(2)}) collective-permute-start(bf16[448,400]{1,0:T(8,128)(2,1)} %get-tuple-element.33), channel_id=1, source_target_pairs={{0,128},{32,160},{64,192},{96,224},{128,256},{160,288},{192,320},{... | collective-permute-start | bytes 1075208 | tf_op jit(solution)/shard_map/ppermute | solution.py:98
  96.8 1.9 collective-permute-start.6
  118.4 2.4 pad_maximum_fusion.1
  121.5 1.9 collective-permute-start.7
  124.3 5.8 %collective-permute-start.8 = (bf16[448,400]{1,0:T(8,128)(2,1)S(1)}, bf16[448,400]{1,0:T(8,128)(2,1)S(1)}, u32[]{:S(2)}, u32[]{:S(2)}) collective-permute-start(bf16[448,400]{1,0:T(8,128)(2,1)S(1)} %copy-done.5), channel_id=1, source_target_pairs={{0,224},{32,256},{64,288},{96,320},{128,352},{160,384},{192,416},{... | collective-permute-start | bytes 1075208 | tf_op jit(solution)/shard_map/ppermute | solution.py:98
  130.8 3.7 collective-permute-start.9
  135.4 4.7 %collective-permute-start.10 = (bf16[448,400]{1,0:T(8,128)(2,1)S(1)}, bf16[448,400]{1,0:T(8,128)(2,1)S(1)}, u32[]{:S(2)}, u32[]{:S(2)}) collective-permute-start(bf16[448,400]{1,0:T(8,128)(2,1)S(1)} %get-tuple-element.39), channel_id=1, source_target_pairs={{0,288},{32,320},{64,352},{96,384},{128,416},{160,448},{192,480},{... | collective-permute-start | bytes 1075208 | tf_op jit(solution)/shard_map/ppermute | solution.py:98
  140.9 33.3 %collective-permute-start.11 = (bf16[448,400]{1,0:T(8,128)(2,1)S(1)}, bf16[448,400]{1,0:T(8,128)(2,1)S(1)}, u32[]{:S(2)}, u32[]{:S(2)}) collective-permute-start(bf16[448,400]{1,0:T(8,128)(2,1)S(1)} %get-tuple-element.40), channel_id=1, source_target_pairs={{0,320},{32,352},{64,384},{96,416},{128,448},{160,480},{192,0},{22... | collective-permute-start | bytes 1075208 | tf_op jit(solution)/shard_map/ppermute | solution.py:98
  175.1 8.1 %collective-permute-start.12 = (bf16[448,400]{1,0:T(8,128)(2,1)S(1)}, bf16[448,400]{1,0:T(8,128)(2,1)S(1)}, u32[]{:S(2)}, u32[]{:S(2)}) collective-permute-start(bf16[448,400]{1,0:T(8,128)(2,1)S(1)} %get-tuple-element.41), channel_id=1, source_target_pairs={{0,352},{32,384},{64,416},{96,448},{128,480},{160,0},{192,32},{224... | collective-permute-start | bytes 1075208 | tf_op jit(solution)/shard_map/ppermute | solution.py:98
  186.7 6.9 %collective-permute-start.14 = (bf16[448,400]{1,0:T(8,128)(2,1)S(1)}, bf16[448,400]{1,0:T(8,128)(2,1)S(1)}, u32[]{:S(2)}, u32[]{:S(2)}) collective-permute-start(bf16[448,400]{1,0:T(8,128)(2,1)S(1)} %get-tuple-element.43), channel_id=1, source_target_pairs={{0,416},{32,448},{64,480},{96,0},{128,32},{160,64},{192,96},{224,1... | collective-permute-start | bytes 1075208 | tf_op jit(solution)/shard_map/ppermute | solution.py:98
  194.4 2.2 collective-permute-start.15
  197.4 4.2 %collective-permute-start.16 = (bf16[448,400]{1,0:T(8,128)(2,1)S(1)}, bf16[448,400]{1,0:T(8,128)(2,1)S(1)}, u32[]{:S(2)}, u32[]{:S(2)}) collective-permute-start(bf16[448,400]{1,0:T(8,128)(2,1)S(1)} %copy-done.3), channel_id=1, source_target_pairs={{0,480},{32,0},{64,32},{96,64},{128,96},{160,128},{192,160},{224,1... | collective-permute-start | bytes 1075208 | tf_op jit(solution)/shard_map/ppermute | solution.py:98
  203.3 8.2 %collective-permute-done.13 = bf16[448,400]{1,0:T(8,128)(2,1)S(1)} collective-permute-done((bf16[448,400]{1,0:T(8,128)(2,1)S(1)}, bf16[448,400]{1,0:T(8,128)(2,1)S(1)}, u32[]{:S(2)}, u32[]{:S(2)}) %collective-permute-start.13) | collective-permute-done | bytes 358432 | tf_op jit(solution)/shard_map/ppermute | solution.py:98
  212.3 9.0 %collective-permute-done.14 = bf16[448,400]{1,0:T(8,128)(2,1)S(1)} collective-permute-done((bf16[448,400]{1,0:T(8,128)(2,1)S(1)}, bf16[448,400]{1,0:T(8,128)(2,1)S(1)}, u32[]{:S(2)}, u32[]{:S(2)}) %collective-permute-start.14) | collective-permute-done | bytes 358432 | tf_op jit(solution)/shard_map/ppermute | solution.py:98
  222.1 9.0 %collective-permute-done.15 = bf16[448,400]{1,0:T(8,128)(2,1)S(1)} collective-permute-done((bf16[448,400]{1,0:T(8,128)(2,1)S(1)}, bf16[448,400]{1,0:T(8,128)(2,1)S(1)}, u32[]{:S(2)}, u32[]{:S(2)}) %collective-permute-start.15) | collective-permute-done | bytes 358432 | tf_op jit(solution)/shard_map/ppermute | solution.py:98
  231.9 9.0 %collective-permute-done.16 = bf16[448,400]{1,0:T(8,128)(2,1)S(1)} collective-permute-done((bf16[448,400]{1,0:T(8,128)(2,1)S(1)}, bf16[448,400]{1,0:T(8,128)(2,1)S(1)}, u32[]{:S(2)}, u32[]{:S(2)}) %collective-permute-start.16) | collective-permute-done | bytes 358432 | tf_op jit(solution)/shard_map/ppermute | solution.py:98
  241.7 1.9 slice.45
  243.6 3.8 convert_bitcast_fusion
  247.5 2.5 fusion
  250.0 2.2 multiply_reduce_fusion
  253.4 7.3 %reshape.244 = f32[160,16,448]{2,1,0:T(8,128)} reshape(f32[2,80,32,224]{3,2,1,0:T(8,128)} %convert_bitcast_fusion) | data formatting | bytes 9175040 | tf_op jit(solution)/shard_map/convert_element_type | solution.py:127
  261.0 3.1 add_convert_fusion
  264.0 5.2 %rev.6 = bf16[160,16,448]{2,1,0:T(8,128)(2,1)} reverse(bf16[160,16,448]{2,1,0:T(8,128)(2,1)S(1)} %add_convert_fusion), dimensions={1} | reverse | bytes 4587520 | tf_op jit(solution)/shard_map/rev | solution.py:56
  269.2 5.8 %fusion.1 = bf16[160,16,448]{2,1,0:T(8,128)(2,1)} fusion(s32[]{:T(128)S(6)} %select_n.270, bf16[160,16,448]{2,1,0:T(8,128)(2,1)} %rev.6), kind=kLoop, calls=%fused_computation.7 | loop fusion | flops 4587520 | bytes 4587524 | tf_op jit(solution)/shard_map/concatenate | solution.py:57
  275.0 4.6 %reshape.240 = bf16[160,7168]{1,0:T(8,128)(2,1)S(1)} reshape(bf16[160,16,448]{2,1,0:T(8,128)(2,1)} %fusion.1) | data formatting | bytes 4587520 | tf_op jit(solution)/shard_map/reshape | solution.py:59
  279.7 4.4 %fusion.42 = f32[160,400]{1,0:T(8,128)S(1)} fusion(bf16[160,7168]{1,0:T(8,128)(2,1)S(1)} %reshape.240, bf16[7168,400]{1,0:T(8,128)(2,1)} %constant_dynamic-update-slice_fusion), kind=kOutput, calls=%fused_computation.151 | convolution fusion | flops 917504000 | bytes 8284160 | tf_op jit(solution)/shard_map/dot_general | solution.py:138
  286.3 1.9 collective-permute-start.17
  288.2 4.2 %collective-permute-start.18 = (bf16[256,224]{0,1:T(8,128)(2,1)S(1)}, bf16[256,224]{0,1:T(8,128)(2,1)S(1)}, u32[]{:S(2)}, u32[]{:S(2)}) collective-permute-start(bf16[256,224]{0,1:T(8,128)(2,1)S(1)} %copy-done.7), channel_id=1, source_target_pairs={{0,64},{32,96},{64,128},{96,160},{128,192},{160,224},{192,256},{22... | collective-permute-start | bytes 344072 | tf_op jit(solution)/shard_map/ppermute | solution.py:98
  292.4 1.9 collective-permute-start.19
  294.4 5.6 %collective-permute-start.20 = (bf16[256,224]{0,1:T(8,128)(2,1)S(1)}, bf16[256,224]{0,1:T(8,128)(2,1)S(1)}, u32[]{:S(2)}, u32[]{:S(2)}) collective-permute-start(bf16[256,224]{0,1:T(8,128)(2,1)S(1)} %copy-done.7), channel_id=1, source_target_pairs={{0,128},{32,160},{64,192},{96,224},{128,256},{160,288},{192,320},{... | collective-permute-start | bytes 344072 | tf_op jit(solution)/shard_map/ppermute | solution.py:98
  299.9 4.7 %collective-permute-start.21 = (bf16[256,224]{0,1:T(8,128)(2,1)S(1)}, bf16[256,224]{0,1:T(8,128)(2,1)S(1)}, u32[]{:S(2)}, u32[]{:S(2)}) collective-permute-start(bf16[256,224]{0,1:T(8,128)(2,1)S(1)} %copy-done.7), channel_id=1, source_target_pairs={{0,160},{32,192},{64,224},{96,256},{128,288},{160,320},{192,352},{... | collective-permute-start | bytes 344072 | tf_op jit(solution)/shard_map/ppermute | solution.py:98
  307.9 5.5 %collective-permute-start.23 = (bf16[256,224]{0,1:T(8,128)(2,1)S(1)}, bf16[256,224]{0,1:T(8,128)(2,1)S(1)}, u32[]{:S(2)}, u32[]{:S(2)}) collective-permute-start(bf16[256,224]{0,1:T(8,128)(2,1)S(1)} %copy-done.7), channel_id=1, source_target_pairs={{0,224},{32,256},{64,288},{96,320},{128,352},{160,384},{192,416},{... | collective-permute-start | bytes 344072 | tf_op jit(solution)/shard_map/ppermute | solution.py:98
  314.0 4.0 %collective-permute-start.24 = (bf16[256,224]{0,1:T(8,128)(2,1)S(1)}, bf16[256,224]{0,1:T(8,128)(2,1)S(1)}, u32[]{:S(2)}, u32[]{:S(2)}) collective-permute-start(bf16[256,224]{0,1:T(8,128)(2,1)S(1)} %copy-done.7), channel_id=1, source_target_pairs={{0,256},{32,288},{64,320},{96,352},{128,384},{160,416},{192,448},{... | collective-permute-start | bytes 344072 | tf_op jit(solution)/shard_map/ppermute | solution.py:98
  318.7 2.8 collective-permute-start.25
  322.2 6.6 %collective-permute-start.26 = (bf16[256,224]{0,1:T(8,128)(2,1)S(1)}, bf16[256,224]{0,1:T(8,128)(2,1)S(1)}, u32[]{:S(2)}, u32[]{:S(2)}) collective-permute-start(bf16[256,224]{0,1:T(8,128)(2,1)S(1)} %copy-done.7), channel_id=1, source_target_pairs={{0,320},{32,352},{64,384},{96,416},{128,448},{160,480},{192,0},{22... | collective-permute-start | bytes 344072 | tf_op jit(solution)/shard_map/ppermute | solution.py:98
  329.4 3.5 collective-permute-start.27
  333.6 3.1 collective-permute-start.28
  337.4 2.4 collective-permute-start.29
  340.5 1.9 collective-permute-start.30
  343.2 4.8 %collective-permute-start.31 = (bf16[256,224]{0,1:T(8,128)(2,1)S(1)}, bf16[256,224]{0,1:T(8,128)(2,1)S(1)}, u32[]{:S(2)}, u32[]{:S(2)}) collective-permute-start(bf16[256,224]{0,1:T(8,128)(2,1)S(1)} %copy-done.7), channel_id=1, source_target_pairs={{0,480},{32,0},{64,32},{96,64},{128,96},{160,128},{192,160},{224,1... | collective-permute-start | bytes 344072 | tf_op jit(solution)/shard_map/ppermute | solution.py:98
  352.0 14.3 %all-gather.7.cloned.1.call-done = bf16[5632,128]{1,0:T(8,128)(2,1)} async-done(((bf16[176,128]{1,0:T(8,128)(2,1)}), bf16[5632,128]{1,0:T(8,128)(2,1)}) %all-gather.7.cloned.1.call-update) | async-done | bytes 1441808 | tf_op jit(solution)/shard_map/all_gather | solution.py:159
  371.6 2.1 fusion.8
  373.6 2.9 fusion.5
  (166 shorter events, 64.2 us)
Async XLA Ops:
  6.5 277.6 %copy-start = (bf16[64,16,384]{2,1,0:T(8,128)(2,1)S(1)}, bf16[64,16,384]{2,1,0:T(8,128)(2,1)}, u32[]{:S(2)}) copy-start(bf16[64,16,384]{2,1,0:T(8,128)(2,1)} %param.24) | copy-start | bytes 2359300
  6.5 48.8 %copy-start.1 = (bf16[448,384]{1,0:T(8,128)(2,1)S(1)}, bf16[448,384]{1,0:T(8,128)(2,1)}, u32[]{:S(2)}) copy-start(bf16[448,384]{1,0:T(8,128)(2,1)} %param.19) | copy-start | bytes 1032196
  6.5 235.2 %all-gather.5.cloned.1.call-start = ((), (), s32[]{:S(2)}) async-start(), calls=%async_computation | async-start | bytes 2973696 | tf_op jit(solution)/shard_map/all_gather | solution.py:120
  9.0 9.4 %collective-permute-start = (bf16[82,224]{1,0:T(8,128)(2,1)S(1)}, bf16[82,224]{1,0:T(8,128)(2,1)S(1)}, u32[]{:S(2)}, u32[]{:S(2)}) collective-permute-start(bf16[82,224]{1,0:T(8,128)(2,1)S(1)} %get-tuple-element.49), channel_id=1, source_target_pairs={{0,0},{1,1},{2,32},{3,33},{4,64},{5,65},{6,96},{7,97},{8,128},{9,1... | collective-permute-start | bytes 110216 | tf_op jit(solution)/shard_map/ppermute | solution.py:116
  9.7 9.6 %collective-permute-start.1 = (bf16[82,224]{1,0:T(8,128)(2,1)S(1)}, bf16[82,224]{1,0:T(8,128)(2,1)S(1)}, u32[]{:S(2)}, u32[]{:S(2)}) collective-permute-start(bf16[82,224]{1,0:T(8,128)(2,1)S(1)} %get-tuple-element.50), channel_id=1, source_target_pairs={{0,1},{1,0},{2,33},{3,32},{4,65},{5,64},{6,97},{7,96},{8,129},{9,1... | collective-permute-start | bytes 110216 | tf_op jit(solution)/shard_map/ppermute | solution.py:116
  20.0 346.4 %all-gather.7.cloned.1.call-start = ((), (), s32[]{:S(2)}) async-start(), calls=%async_computation.1 | async-start | bytes 1486848 | tf_op jit(solution)/shard_map/all_gather | solution.py:159
  55.4 43.4 %copy-start.15 = (s32[16]{0:T(128)S(1)}, s32[16]{0:T(128)}, u32[]{:S(2)}) copy-start(s32[16]{0:T(128)} %param.29) | copy-start | bytes 196
  55.4 45.5 %copy-start.16 = (s32[16]{0:T(128)S(1)}, s32[16]{0:T(128)}, u32[]{:S(2)}) copy-start(s32[16]{0:T(128)} %param.27) | copy-start | bytes 196
  57.6 63.9 %collective-permute-start.2 = (bf16[448,400]{1,0:T(8,128)(2,1)}, bf16[448,400]{1,0:T(8,128)(2,1)S(1)}, u32[]{:S(2)}, u32[]{:S(2)}) collective-permute-start(bf16[448,400]{1,0:T(8,128)(2,1)} %get-tuple-element.30), channel_id=1, source_target_pairs={{0,32},{32,64},{64,96},{96,128},{128,160},{160,192},{192,224},{224... | collective-permute-start | bytes 1075208 | tf_op jit(solution)/shard_map/ppermute | solution.py:98
  64.4 59.9 %collective-permute-start.3 = (bf16[448,400]{1,0:T(8,128)(2,1)}, bf16[448,400]{1,0:T(8,128)(2,1)S(1)}, u32[]{:S(2)}, u32[]{:S(2)}) collective-permute-start(bf16[448,400]{1,0:T(8,128)(2,1)} %get-tuple-element.31), channel_id=1, source_target_pairs={{0,64},{32,96},{64,128},{96,160},{128,192},{160,224},{192,256},{22... | collective-permute-start | bytes 1075208 | tf_op jit(solution)/shard_map/ppermute | solution.py:98
  72.5 58.4 %collective-permute-start.4 = (bf16[448,400]{1,0:T(8,128)(2,1)}, bf16[448,400]{1,0:T(8,128)(2,1)S(1)}, u32[]{:S(2)}, u32[]{:S(2)}) collective-permute-start(bf16[448,400]{1,0:T(8,128)(2,1)} %get-tuple-element.32), channel_id=1, source_target_pairs={{0,96},{32,128},{64,160},{96,192},{128,224},{160,256},{192,288},{2... | collective-permute-start | bytes 1075208 | tf_op jit(solution)/shard_map/ppermute | solution.py:98
  86.0 49.4 %collective-permute-start.5 = (bf16[448,400]{1,0:T(8,128)(2,1)}, bf16[448,400]{1,0:T(8,128)(2,1)S(1)}, u32[]{:S(2)}, u32[]{:S(2)}) collective-permute-start(bf16[448,400]{1,0:T(8,128)(2,1)} %get-tuple-element.33), channel_id=1, source_target_pairs={{0,128},{32,160},{64,192},{96,224},{128,256},{160,288},{192,320},{... | collective-permute-start | bytes 1075208 | tf_op jit(solution)/shard_map/ppermute | solution.py:98
  96.8 44.1 %collective-permute-start.6 = (bf16[448,400]{1,0:T(8,128)(2,1)}, bf16[448,400]{1,0:T(8,128)(2,1)S(1)}, u32[]{:S(2)}, u32[]{:S(2)}) collective-permute-start(bf16[448,400]{1,0:T(8,128)(2,1)} %get-tuple-element.34), channel_id=1, source_target_pairs={{0,160},{32,192},{64,224},{96,256},{128,288},{160,320},{192,352},{... | collective-permute-start | bytes 1075208 | tf_op jit(solution)/shard_map/ppermute | solution.py:98
  118.4 5.9 %copy-start.5 = (bf16[448,400]{1,0:T(8,128)(2,1)S(1)}, bf16[448,400]{1,0:T(8,128)(2,1)}, u32[]{:S(2)}) copy-start(bf16[448,400]{1,0:T(8,128)(2,1)} %get-tuple-element.36) | copy-start | bytes 1075204
  118.4 12.4 %copy-start.4 = (bf16[448,400]{1,0:T(8,128)(2,1)S(1)}, bf16[448,400]{1,0:T(8,128)(2,1)}, u32[]{:S(2)}) copy-start(bf16[448,400]{1,0:T(8,128)(2,1)} %get-tuple-element.37) | copy-start | bytes 1075204
  121.5 53.5 %collective-permute-start.7 = (bf16[448,400]{1,0:T(8,128)(2,1)S(1)}, bf16[448,400]{1,0:T(8,128)(2,1)S(1)}, u32[]{:S(2)}, u32[]{:S(2)}) collective-permute-start(bf16[448,400]{1,0:T(8,128)(2,1)S(1)} %copy-done.6), channel_id=1, source_target_pairs={{0,192},{32,224},{64,256},{96,288},{128,320},{160,352},{192,384},{... | collective-permute-start | bytes 1075208 | tf_op jit(solution)/shard_map/ppermute | solution.py:98
  124.3 59.7 %collective-permute-start.8 = (bf16[448,400]{1,0:T(8,128)(2,1)S(1)}, bf16[448,400]{1,0:T(8,128)(2,1)S(1)}, u32[]{:S(2)}, u32[]{:S(2)}) collective-permute-start(bf16[448,400]{1,0:T(8,128)(2,1)S(1)} %copy-done.5), channel_id=1, source_target_pairs={{0,224},{32,256},{64,288},{96,320},{128,352},{160,384},{192,416},{... | collective-permute-start | bytes 1075208 | tf_op jit(solution)/shard_map/ppermute | solution.py:98
  130.8 55.9 %collective-permute-start.9 = (bf16[448,400]{1,0:T(8,128)(2,1)S(1)}, bf16[448,400]{1,0:T(8,128)(2,1)S(1)}, u32[]{:S(2)}, u32[]{:S(2)}) collective-permute-start(bf16[448,400]{1,0:T(8,128)(2,1)S(1)} %copy-done.4), channel_id=1, source_target_pairs={{0,256},{32,288},{64,320},{96,352},{128,384},{160,416},{192,448},{... | collective-permute-start | bytes 1075208 | tf_op jit(solution)/shard_map/ppermute | solution.py:98
  135.4 62.0 %copy-start.3 = (bf16[448,400]{1,0:T(8,128)(2,1)S(1)}, bf16[448,400]{1,0:T(8,128)(2,1)}, u32[]{:S(2)}) copy-start(bf16[448,400]{1,0:T(8,128)(2,1)} %get-tuple-element.29) | copy-start | bytes 1075204
  135.4 59.0 %collective-permute-start.10 = (bf16[448,400]{1,0:T(8,128)(2,1)S(1)}, bf16[448,400]{1,0:T(8,128)(2,1)S(1)}, u32[]{:S(2)}, u32[]{:S(2)}) collective-permute-start(bf16[448,400]{1,0:T(8,128)(2,1)S(1)} %get-tuple-element.39), channel_id=1, source_target_pairs={{0,288},{32,320},{64,352},{96,384},{128,416},{160,448},{192,480},{... | collective-permute-start | bytes 1075208 | tf_op jit(solution)/shard_map/ppermute | solution.py:98
  140.9 56.5 %collective-permute-start.11 = (bf16[448,400]{1,0:T(8,128)(2,1)S(1)}, bf16[448,400]{1,0:T(8,128)(2,1)S(1)}, u32[]{:S(2)}, u32[]{:S(2)}) collective-permute-start(bf16[448,400]{1,0:T(8,128)(2,1)S(1)} %get-tuple-element.40), channel_id=1, source_target_pairs={{0,320},{32,352},{64,384},{96,416},{128,448},{160,480},{192,0},{22... | collective-permute-start | bytes 1075208 | tf_op jit(solution)/shard_map/ppermute | solution.py:98
  175.1 27.4 %collective-permute-start.12 = (bf16[448,400]{1,0:T(8,128)(2,1)S(1)}, bf16[448,400]{1,0:T(8,128)(2,1)S(1)}, u32[]{:S(2)}, u32[]{:S(2)}) collective-permute-start(bf16[448,400]{1,0:T(8,128)(2,1)S(1)} %get-tuple-element.41), channel_id=1, source_target_pairs={{0,352},{32,384},{64,416},{96,448},{128,480},{160,0},{192,32},{224... | collective-permute-start | bytes 1075208 | tf_op jit(solution)/shard_map/ppermute | solution.py:98
  184.0 27.5 %collective-permute-start.13 = (bf16[448,400]{1,0:T(8,128)(2,1)S(1)}, bf16[448,400]{1,0:T(8,128)(2,1)S(1)}, u32[]{:S(2)}, u32[]{:S(2)}) collective-permute-start(bf16[448,400]{1,0:T(8,128)(2,1)S(1)} %get-tuple-element.42), channel_id=1, source_target_pairs={{0,384},{32,416},{64,448},{96,480},{128,0},{160,32},{192,64},{224,... | collective-permute-start | bytes 1075208 | tf_op jit(solution)/shard_map/ppermute | solution.py:98
  186.7 34.6 %collective-permute-start.14 = (bf16[448,400]{1,0:T(8,128)(2,1)S(1)}, bf16[448,400]{1,0:T(8,128)(2,1)S(1)}, u32[]{:S(2)}, u32[]{:S(2)}) collective-permute-start(bf16[448,400]{1,0:T(8,128)(2,1)S(1)} %get-tuple-element.43), channel_id=1, source_target_pairs={{0,416},{32,448},{64,480},{96,0},{128,32},{160,64},{192,96},{224,1... | collective-permute-start | bytes 1075208 | tf_op jit(solution)/shard_map/ppermute | solution.py:98
  194.4 36.7 %collective-permute-start.15 = (bf16[448,400]{1,0:T(8,128)(2,1)S(1)}, bf16[448,400]{1,0:T(8,128)(2,1)S(1)}, u32[]{:S(2)}, u32[]{:S(2)}) collective-permute-start(bf16[448,400]{1,0:T(8,128)(2,1)S(1)} %get-tuple-element.38), channel_id=1, source_target_pairs={{0,448},{32,480},{64,0},{96,32},{128,64},{160,96},{192,128},{224,1... | collective-permute-start | bytes 1075208 | tf_op jit(solution)/shard_map/ppermute | solution.py:98
  197.4 43.5 %collective-permute-start.16 = (bf16[448,400]{1,0:T(8,128)(2,1)S(1)}, bf16[448,400]{1,0:T(8,128)(2,1)S(1)}, u32[]{:S(2)}, u32[]{:S(2)}) collective-permute-start(bf16[448,400]{1,0:T(8,128)(2,1)S(1)} %copy-done.3), channel_id=1, source_target_pairs={{0,480},{32,0},{64,32},{96,64},{128,96},{160,128},{192,160},{224,1... | collective-permute-start | bytes 1075208 | tf_op jit(solution)/shard_map/ppermute | solution.py:98
  279.6 5.1 %copy-start.8 = (s32[160]{0:T(256)S(1)}, s32[160]{0:T(256)}, u32[]{:S(2)}) copy-start(s32[160]{0:T(256)} %get-tuple-element.52) | copy-start | bytes 1924
  279.6 5.1 %copy-start.9 = (s32[160]{0:T(256)S(1)}, s32[160]{0:T(256)}, u32[]{:S(2)}) copy-start(s32[160]{0:T(256)} %get-tuple-element.12) | copy-start | bytes 1924
  279.6 5.1 %copy-start.10 = (pred[160]{0:T(512)(128)(4,1)S(1)}, pred[160]{0:T(512)(128)(4,1)}, u32[]{:S(2)}) copy-start(pred[160]{0:T(512)(128)(4,1)} %get-tuple-element.8) | copy-start | bytes 484
  279.6 5.1 %copy-start.12 = (pred[160]{0:T(512)(128)(4,1)S(1)}, pred[160]{0:T(512)(128)(4,1)}, u32[]{:S(2)}) copy-start(pred[160]{0:T(512)(128)(4,1)} %get-tuple-element.51) | copy-start | bytes 484
  279.7 5.1 %copy-start.13 = (pred[160]{0:T(512)(128)(4,1)S(1)}, pred[160]{0:T(512)(128)(4,1)}, u32[]{:S(2)}) copy-start(pred[160]{0:T(512)(128)(4,1)} %get-tuple-element.11) | copy-start | bytes 484
  279.7 5.1 %copy-start.14 = (pred[160]{0:T(512)(128)(4,1)S(1)}, pred[160]{0:T(512)(128)(4,1)}, u32[]{:S(2)}) copy-start(pred[160]{0:T(512)(128)(4,1)} %get-tuple-element.72) | copy-start | bytes 484
  284.1 20.5 %copy-start.17 = (bf16[224]{0:T(256)(128)(2,1)S(1)}, bf16[224]{0:T(256)(128)(2,1)}, u32[]{:S(2)}) copy-start(bf16[224]{0:T(256)(128)(2,1)} %param.22) | copy-start | bytes 1348
  286.3 19.0 %collective-permute-start.17 = (bf16[256,224]{0,1:T(8,128)(2,1)S(1)}, bf16[256,224]{0,1:T(8,128)(2,1)S(1)}, u32[]{:S(2)}, u32[]{:S(2)}) collective-permute-start(bf16[256,224]{0,1:T(8,128)(2,1)S(1)} %copy-done.7), channel_id=1, source_target_pairs={{0,32},{32,64},{64,96},{96,128},{128,160},{160,192},{192,224},{224... | collective-permute-start | bytes 344072 | tf_op jit(solution)/shard_map/ppermute | solution.py:98
  288.2 19.7 %collective-permute-start.18 = (bf16[256,224]{0,1:T(8,128)(2,1)S(1)}, bf16[256,224]{0,1:T(8,128)(2,1)S(1)}, u32[]{:S(2)}, u32[]{:S(2)}) collective-permute-start(bf16[256,224]{0,1:T(8,128)(2,1)S(1)} %copy-done.7), channel_id=1, source_target_pairs={{0,64},{32,96},{64,128},{96,160},{128,192},{160,224},{192,256},{22... | collective-permute-start | bytes 344072 | tf_op jit(solution)/shard_map/ppermute | solution.py:98
  292.4 21.6 %collective-permute-start.19 = (bf16[256,224]{0,1:T(8,128)(2,1)S(1)}, bf16[256,224]{0,1:T(8,128)(2,1)S(1)}, u32[]{:S(2)}, u32[]{:S(2)}) collective-permute-start(bf16[256,224]{0,1:T(8,128)(2,1)S(1)} %copy-done.7), channel_id=1, source_target_pairs={{0,96},{32,128},{64,160},{96,192},{128,224},{160,256},{192,288},{2... | collective-permute-start | bytes 344072 | tf_op jit(solution)/shard_map/ppermute | solution.py:98
  294.4 24.4 %collective-permute-start.20 = (bf16[256,224]{0,1:T(8,128)(2,1)S(1)}, bf16[256,224]{0,1:T(8,128)(2,1)S(1)}, u32[]{:S(2)}, u32[]{:S(2)}) collective-permute-start(bf16[256,224]{0,1:T(8,128)(2,1)S(1)} %copy-done.7), channel_id=1, source_target_pairs={{0,128},{32,160},{64,192},{96,224},{128,256},{160,288},{192,320},{... | collective-permute-start | bytes 344072 | tf_op jit(solution)/shard_map/ppermute | solution.py:98
  299.9 22.2 %collective-permute-start.21 = (bf16[256,224]{0,1:T(8,128)(2,1)S(1)}, bf16[256,224]{0,1:T(8,128)(2,1)S(1)}, u32[]{:S(2)}, u32[]{:S(2)}) collective-permute-start(bf16[256,224]{0,1:T(8,128)(2,1)S(1)} %copy-done.7), channel_id=1, source_target_pairs={{0,160},{32,192},{64,224},{96,256},{128,288},{160,320},{192,352},{... | collective-permute-start | bytes 344072 | tf_op jit(solution)/shard_map/ppermute | solution.py:98
  305.3 24.1 %collective-permute-start.22 = (bf16[256,224]{0,1:T(8,128)(2,1)S(1)}, bf16[256,224]{0,1:T(8,128)(2,1)S(1)}, u32[]{:S(2)}, u32[]{:S(2)}) collective-permute-start(bf16[256,224]{0,1:T(8,128)(2,1)S(1)} %copy-done.7), channel_id=1, source_target_pairs={{0,192},{32,224},{64,256},{96,288},{128,320},{160,352},{192,384},{... | collective-permute-start | bytes 344072 | tf_op jit(solution)/shard_map/ppermute | solution.py:98
  307.9 25.7 %collective-permute-start.23 = (bf16[256,224]{0,1:T(8,128)(2,1)S(1)}, bf16[256,224]{0,1:T(8,128)(2,1)S(1)}, u32[]{:S(2)}, u32[]{:S(2)}) collective-permute-start(bf16[256,224]{0,1:T(8,128)(2,1)S(1)} %copy-done.7), channel_id=1, source_target_pairs={{0,224},{32,256},{64,288},{96,320},{128,352},{160,384},{192,416},{... | collective-permute-start | bytes 344072 | tf_op jit(solution)/shard_map/ppermute | solution.py:98
  314.0 23.3 %collective-permute-start.24 = (bf16[256,224]{0,1:T(8,128)(2,1)S(1)}, bf16[256,224]{0,1:T(8,128)(2,1)S(1)}, u32[]{:S(2)}, u32[]{:S(2)}) collective-permute-start(bf16[256,224]{0,1:T(8,128)(2,1)S(1)} %copy-done.7), channel_id=1, source_target_pairs={{0,256},{32,288},{64,320},{96,352},{128,384},{160,416},{192,448},{... | collective-permute-start | bytes 344072 | tf_op jit(solution)/shard_map/ppermute | solution.py:98
  318.7 21.8 %collective-permute-start.25 = (bf16[256,224]{0,1:T(8,128)(2,1)S(1)}, bf16[256,224]{0,1:T(8,128)(2,1)S(1)}, u32[]{:S(2)}, u32[]{:S(2)}) collective-permute-start(bf16[256,224]{0,1:T(8,128)(2,1)S(1)} %copy-done.7), channel_id=1, source_target_pairs={{0,288},{32,320},{64,352},{96,384},{128,416},{160,448},{192,480},{... | collective-permute-start | bytes 344072 | tf_op jit(solution)/shard_map/ppermute | solution.py:98
  322.2 21.0 %collective-permute-start.26 = (bf16[256,224]{0,1:T(8,128)(2,1)S(1)}, bf16[256,224]{0,1:T(8,128)(2,1)S(1)}, u32[]{:S(2)}, u32[]{:S(2)}) collective-permute-start(bf16[256,224]{0,1:T(8,128)(2,1)S(1)} %copy-done.7), channel_id=1, source_target_pairs={{0,320},{32,352},{64,384},{96,416},{128,448},{160,480},{192,0},{22... | collective-permute-start | bytes 344072 | tf_op jit(solution)/shard_map/ppermute | solution.py:98
  329.4 19.2 %collective-permute-start.27 = (bf16[256,224]{0,1:T(8,128)(2,1)S(1)}, bf16[256,224]{0,1:T(8,128)(2,1)S(1)}, u32[]{:S(2)}, u32[]{:S(2)}) collective-permute-start(bf16[256,224]{0,1:T(8,128)(2,1)S(1)} %copy-done.7), channel_id=1, source_target_pairs={{0,352},{32,384},{64,416},{96,448},{128,480},{160,0},{192,32},{224... | collective-permute-start | bytes 344072 | tf_op jit(solution)/shard_map/ppermute | solution.py:98
  333.6 15.7 %collective-permute-start.28 = (bf16[256,224]{0,1:T(8,128)(2,1)S(1)}, bf16[256,224]{0,1:T(8,128)(2,1)S(1)}, u32[]{:S(2)}, u32[]{:S(2)}) collective-permute-start(bf16[256,224]{0,1:T(8,128)(2,1)S(1)} %copy-done.7), channel_id=1, source_target_pairs={{0,384},{32,416},{64,448},{96,480},{128,0},{160,32},{192,64},{224,... | collective-permute-start | bytes 344072 | tf_op jit(solution)/shard_map/ppermute | solution.py:98
  337.4 12.6 %collective-permute-start.29 = (bf16[256,224]{0,1:T(8,128)(2,1)S(1)}, bf16[256,224]{0,1:T(8,128)(2,1)S(1)}, u32[]{:S(2)}, u32[]{:S(2)}) collective-permute-start(bf16[256,224]{0,1:T(8,128)(2,1)S(1)} %copy-done.7), channel_id=1, source_target_pairs={{0,416},{32,448},{64,480},{96,0},{128,32},{160,64},{192,96},{224,1... | collective-permute-start | bytes 344072 | tf_op jit(solution)/shard_map/ppermute | solution.py:98
  340.5 10.1 %collective-permute-start.30 = (bf16[256,224]{0,1:T(8,128)(2,1)S(1)}, bf16[256,224]{0,1:T(8,128)(2,1)S(1)}, u32[]{:S(2)}, u32[]{:S(2)}) collective-permute-start(bf16[256,224]{0,1:T(8,128)(2,1)S(1)} %copy-done.7), channel_id=1, source_target_pairs={{0,448},{32,480},{64,0},{96,32},{128,64},{160,96},{192,128},{224,1... | collective-permute-start | bytes 344072 | tf_op jit(solution)/shard_map/ppermute | solution.py:98
  343.2 8.2 %collective-permute-start.31 = (bf16[256,224]{0,1:T(8,128)(2,1)S(1)}, bf16[256,224]{0,1:T(8,128)(2,1)S(1)}, u32[]{:S(2)}, u32[]{:S(2)}) collective-permute-start(bf16[256,224]{0,1:T(8,128)(2,1)S(1)} %copy-done.7), channel_id=1, source_target_pairs={{0,480},{32,0},{64,32},{96,64},{128,96},{160,128},{192,160},{224,1... | collective-permute-start | bytes 344072 | tf_op jit(solution)/shard_map/ppermute | solution.py:98
  (4 other events, 9.6 us)
Sparse Core Ops, SparseCore 0:
  20.1 93.7 all-gather.4
  286.4 79.8 all-gather.6

commit v2 on v1

--- a/solution.py
+++ b/solution.py
@@ -50,15 +50,6 @@
     return mixed_rows.astype(jnp.bfloat16).reshape(queries.shape[0], -1)
 
 
-def rolled_blocks(x, blocks, shift):
-    rows = x.shape[0]
-    width = x.shape[1] // blocks
-    reversed_blocks = x.reshape(rows, blocks, width)[:, ::-1, :]
-    doubled = jnp.concatenate([reversed_blocks, reversed_blocks], axis=1)
-    picked = lax.dynamic_slice_in_dim(doubled, blocks - 1 - shift, blocks, axis=1)
-    return picked.reshape(rows, blocks * width)
-
-
 def local(
     hidden,
     ln_gain,
@@ -85,23 +76,18 @@
     own_adapter = adapters[row_index]
     tokens_here, features_here = hidden.shape
     chunk = features_here // 2
+    low_rank = down_qkv.shape[2]
+    head_width = qkv_weight.shape[1]
+    out_rows, out_cols = out_weight.shape
 
-    blocks_a = []
-    blocks_b = []
-    for shift in range(row_count):
-        target_adapter = adapters[(row_index + shift) % row_count]
-        payload = (
-            jnp.concatenate([qkv_weight, down_qkv[target_adapter]], axis=1),
-            out_weight,
-        )
-        if shift:
-            payload = lax.ppermute(
-                payload, "row", [(i, (i + shift) % row_count) for i in range(row_count)]
-            )
-        blocks_a.append(payload[0])
-        blocks_b.append(payload[1])
-    weight_a = jnp.concatenate(blocks_a, axis=0)
-    weight_b = jnp.concatenate(blocks_b, axis=0)
+    packed = jnp.concatenate(
+        [qkv_weight, out_weight.reshape(features_here, -1)], axis=1
+    )
+    packed_full = lax.all_gather(packed, "row", axis=0, tiled=True)
+    qkv_full = packed_full[:, :head_width]
+    out_full = packed_full[:, head_width:].reshape(row_count * out_rows, out_cols)
+    down_parts = lax.all_to_all(down_qkv[adapters], "row", 0, 0, tiled=True)
+    down_full = down_parts.reshape(-1, low_rank)
 
     payload = jnp.concatenate([hidden, ln_gain[None], ln_shift[None]], axis=0)
     parity = col_index % 2
@@ -116,13 +102,11 @@
         halves.append(lax.ppermute(sent, ("row", "col"), pairs))
     first = jnp.where(parity == 0, halves[0], halves[1])
     second = jnp.where(parity == 0, halves[1], halves[0])
-    mine = jnp.stack([first, second])
-    gathered = lax.all_gather(mine, "col", axis=0, tiled=False)
-    features = jnp.transpose(gathered[:, :, :tokens_here, :], (1, 2, 0, 3)).reshape(
-        2 * tokens_here, col_count * chunk
-    )
-    gain_full = gathered[:, 0, tokens_here, :].reshape(-1)
-    shift_full = gathered[:, 0, tokens_here + 1, :].reshape(-1)
+    mine = jnp.concatenate([first[:tokens_here], second], axis=0)
+    gathered = lax.all_gather(mine, "col", axis=1, tiled=True)
+    features = gathered[: 2 * tokens_here]
+    gain_full = gathered[2 * tokens_here]
+    shift_full = gathered[2 * tokens_here + 1]
 
     widened = features.astype(jnp.float32)
     average = jnp.mean(widened, axis=1, keepdims=True)
@@ -133,14 +117,10 @@
         + shift_full.astype(jnp.float32)
     ).astype(jnp.bfloat16)
 
-    low_rank = down_qkv.shape[2]
-    head_width = qkv_weight.shape[1]
-    projected_all = jnp.dot(
-        rolled_blocks(normed, row_count, row_index), weight_a, preferred_element_type=jnp.float32
-    )
-    reduced = projected_all[:, head_width:]
+    projected = jnp.dot(normed, qkv_full, preferred_element_type=jnp.float32)
+    reduced = jnp.dot(normed, down_full, preferred_element_type=jnp.float32)
     projected = (
-        projected_all[:, :head_width]
+        projected
         + qkv_bias.astype(jnp.float32)
         + jnp.dot(
             reduced.astype(jnp.bfloat16), up_qkv[own_adapter], preferred_element_type=jnp.float32
@@ -157,16 +137,14 @@
     mixed_rows = attention(queries, key_rows, value_rows, key_mask(live_rows, request_of, position))
     down_here = down_out[own_adapter]
     both = lax.all_gather(
-        jnp.concatenate([mixed_rows, down_here], axis=0), "col", axis=0, tiled=False
+        jnp.concatenate([mixed_rows, down_here], axis=0), "col", axis=1, tiled=True
     )
-    all_heads = jnp.transpose(both[:, :GCAP], (1, 0, 2)).reshape(GCAP, -1)
-    down_full = jnp.transpose(both[:, GCAP:], (1, 0, 2)).reshape(low_rank, -1)
+    all_heads = both[:GCAP]
+    down_out_full = both[GCAP:]
     reduced_out = lax.dot_general(
-        all_heads, down_full, (((1,), (1,)), ((), ())), preferred_element_type=jnp.float32
+        all_heads, down_out_full, (((1,), (1,)), ((), ())), preferred_element_type=jnp.float32
     ).astype(jnp.bfloat16)
-    combined = jnp.dot(
-        rolled_blocks(all_heads, row_count, row_index), weight_b, preferred_element_type=jnp.float32
-    )
+    combined = jnp.dot(all_heads, out_full, preferred_element_type=jnp.float32)
     result = (
         combined
         + out_bias.astype(jnp.float32)

time: 386 us -> 289 us (0.75)
  starting transfers between devices: 178 us -> 40.7 us
  waiting for transfers between devices: 50.5 us -> 184 us
  local copies, waits for them, and re-layouts: 64.2 us -> 22.5 us
  between operations: 45.8 us -> 15.4 us
  other arithmetic: 34.7 us -> 11.6 us
    ppermute x30 -> x0, starting transfers between devices: 169 us -> none  [local(): lax.ppermute(payload, 'row', [(i, (i + shift) % row_count) for i in range...]
    all_gather x1 -> x2, waiting for transfers between devices: 0.01 us -> 116 us  [the longest x1 69.7 us: local(): packed_full = lax.all_gather(packed, 'row', axis=0, tiled=True)]
    all_gather x1, waiting for transfers between devices: 14.3 us -> 67.7 us  [local(): lax.all_gather(jnp.concatenate([mixed_rows, down_here], axis=0), 'col', a...]
    ppermute x30 -> x0, waiting for transfers between devices: 35.3 us -> none  [local(): lax.ppermute(payload, 'row', [(i, (i + shift) % row_count) for i in range...]
    all_to_all x0 -> x1, starting transfers between devices: none -> 31.2 us  [local(): down_parts = lax.all_to_all(down_qkv[adapters], 'row', 0, 0, tiled=True)]
    unnamed x66 -> x16, local copies, waits for them, and re-layouts: 22.1 us -> 6.34 us
    squeeze x17 -> x0, local copies, waits for them, and re-layouts: 11.9 us -> none  [local(): down_qkv[target_adapter]]
    concatenate x4 -> x1, other arithmetic: 11.5 us -> 1.82 us  [local(): jnp.concatenate([qkv_weight, out_weight.reshape(features_here, -1)], axis=1)]
  transfers between devices with their start and end apart: 34 -> 6, of which waited for: 6 -> 4; matrix products, arithmetic and copies ran while one was open for 13% -> 10% of each run, Pallas kernels for 0% -> 0%
where the time goes in v2:
time: 289 us; the launch traced here: 288 us
  waiting for transfers between devices  184 us (64%)
  starting transfers between devices  40.7 us (14%)
  local copies, waits for them, and re-layouts  22.5 us (8%)
  between operations  15.4 us (5%)
  matrix products  13.6 us (5%)
  other arithmetic  11.6 us (4%)
    all_gather x1, waiting for transfers between devices, local(): packed_full = lax.all_gather(packed, 'row', axis=0, tiled=True)  69.7 us
    all_gather x1, waiting for transfers between devices, local(): lax.all_gather(jnp.concatenate([mixed_rows, down_here], axis=0), 'col', a...  67.7 us
    all_gather x1, waiting for transfers between devices, local(): gathered = lax.all_gather(mine, 'col', axis=1, tiled=True)  45.9 us
    all_to_all x1, starting transfers between devices, local(): down_parts = lax.all_to_all(down_qkv[adapters], 'row', 0, 0, tiled=True)  31.2 us
    ppermute x2, starting transfers between devices, local(): halves.append(lax.ppermute(sent, ('row', 'col'), pairs))  9.41 us
    unnamed x16, local copies, waits for them, and re-layouts  6.34 us
  transfers between devices with their start and end apart: 6, of which 4 were waited for; matrix products, arithmetic and copies ran while one was open for 10% of the time, Pallas kernels for 0%

profile of v2, /device:TPU:1, one launch (start us, length us, event | category | flops | bytes accessed | tf_op | source)
XLA Modules:
  0.0 288.1 jit_solution(9225564456309595381)
XLA Ops:
  6.6 0.8 broadcast_in_dim.42
  7.3 0.7 broadcast_in_dim.43
  8.0 0.9 pad_maximum_fusion.1
  8.9 0.1 constant_dynamic-slice_fusion.2
  9.0 0.7 collective-permute-start
  9.7 8.7 %collective-permute-start.1 = (bf16[82,224]{1,0:T(8,128)(2,1)S(1)}, bf16[82,224]{1,0:T(8,128)(2,1)S(1)}, u32[]{:S(2)}, u32[]{:S(2)}) collective-permute-start(bf16[82,224]{1,0:T(8,128)(2,1)S(1)} %get-tuple-element.16), channel_id=1, source_target_pairs={{0,1},{1,0},{2,33},{3,32},{4,65},{5,64},{6,97},{7,96},{8,129},{9,1... | collective-permute-start | bytes 110216 | tf_op jit(solution)/shard_map/ppermute | solution.py:102
  18.5 0.8 collective-permute-done.1
  19.3 0.6 maximum_bitcast_fusion
  20.0 1.0 copy.27
  21.1 0.3 reshape.195
  21.3 1.8 pad_maximum_fusion
  23.3 0.7 gather_fusion
  23.9 1.3 gather_fusion.1
  25.2 31.2 %all-to-all-start = ((bf16[16,448,16]{1,2,0:T(8,128)(2,1)}), bf16[16,448,16]{1,2,0:T(8,128)(2,1)S(1)}, u32[]{:S(2)}, u32[]{:S(2)}) async-start(bf16[16,448,16]{1,2,0:T(8,128)(2,1)} %gather_fusion.1), calls=%async_computation | async-start | bytes 524288 | tf_op jit(solution)/shard_map/all_to_all | solution.py:89
  56.5 0.6 dynamic_slice.29
  58.4 0.6 dynamic_slice.32
  59.0 1.3 compare_select_fusion.3
  60.4 0.6 dynamic_slice.31
  61.7 0.7 dynamic-slice_bitcast_fusion
  62.4 0.7 add_reduce_fusion
  63.1 0.1 convert_reduce_fusion.1
  63.2 1.3 fusion.56
  64.5 0.1 select_reduce_fusion
  64.6 1.2 fusion.62
  65.9 0.6 broadcast_compare_fusion
  66.5 0.2 copy.28
  66.7 1.0 reshape.196
  67.7 45.9 %all-gather.9.cloned.1.call-done = bf16[32,224,162]{1,2,0:T(8,128)(2,1)} async-done(((bf16[1,224,162]{1,2,0:T(8,128)(2,1)}), bf16[32,224,162]{1,2,0:T(8,128)(2,1)}) %all-gather.9.cloned.1.call-update) | async-done | bytes 2322448 | tf_op jit(solution)/shard_map/all_gather | solution.py:106
  113.6 3.9 %copy.26 = bf16[32,224,162]{1,0,2:T(8,128)(2,1)} copy(bf16[32,224,162]{1,2,0:T(8,128)(2,1)} %all-gather.9.cloned.1.call-done) | data formatting | bytes 4644864 | tf_op jit(solution)/shard_map/all_gather | solution.py:106
  117.5 5.3 %reshape.220 = bf16[7168,162]{0,1:T(8,128)(2,1)S(1)} reshape(bf16[32,224,162]{1,0,2:T(8,128)(2,1)} %copy.26) | data formatting | bytes 4644864
  122.8 0.4 convert_reduce_fusion
  123.2 0.8 fusion.4
  124.0 0.6 add_rsqrt_fusion
  124.6 69.7 %all-gather.5.cloned.1.call-done = bf16[7168,512]{1,0:T(8,128)(2,1)} async-done(((bf16[448,512]{1,0:T(8,128)(2,1)}), bf16[7168,512]{1,0:T(8,128)(2,1)}) %all-gather.5.cloned.1.call-update) | async-done | bytes 7340048 | tf_op jit(solution)/shard_map/all_gather | solution.py:86
  194.3 4.7 %fusion.8 = f32[160,384]{1,0:T(8,128)} fusion(bf16[7168,512]{1,0:T(8,128)(2,1)} %all-gather.5.cloned.1.call-done, f32[384]{0:T(512)S(1)} %convert_element_type.74, f32[7168]{0:T(1024)S(1)} %bitcast.62, f32[7168]{0:T(1024)S(1)} %bitcast.60, f32[160]{0:T(256)} %add_rsqrt_fusion, f32[160]{0:T(256)S(1)} %broadcast_multiply_fusion, ...), kind=kOutput, calls=%fused_computation.13 | convolution fusion | flops 887746560 | bytes 8105984 | tf_op jit(solution)/shard_map/dot_general | solution.py:120
  199.0 3.0 %convolution_add_fusion = f32[160,384]{1,0:T(8,128)} fusion(f32[160,384]{1,0:T(8,128)} %fusion.8, bf16[7168,16]{0,1:T(8,128)(2,1)} %reshape.196, bf16[64,16,384]{2,1,0:T(8,128)(2,1)} %param.24, s32[]{:T(128)S(6)} %select_n.119, f32[7168]{0:T(1024)S(1)} %bitcast.63, f32[7168]{0:T(1024)S(1)} %bitcast.61, f32[160]{0:T(256)} %add_rsqrt_fusion, ...), kind=kOutput, calls=%fused_computation.12 | convolution fusion | flops 45611520 | bytes 3086340 | tf_op jit(solution)/shard_map/dot_general | solution.py:125
  202.1 1.1 reshape.197
  203.2 0.1 fusion.40
  203.3 0.2 fusion.64
  203.4 0.2 fusion.65
  203.7 0.2 fusion.39
  203.9 0.4 fusion.27
  204.3 0.6 pad_maximum_fusion.2
  205.0 0.4 slice-done
  205.4 3.2 %reshape.199 = bf16[4096,224]{1,0:T(8,128)(2,1)} reshape(bf16[7168,128]{1,0:T(8,128)(2,1)S(1)} %slice-done) | data formatting | bytes 3670016 | tf_op jit(solution)/shard_map/reshape | solution.py:88
  208.6 67.7 %all-gather.7.cloned.1.call-done = bf16[176,4096]{1,0:T(8,128)(2,1)} async-done(((bf16[176,128]{1,0:T(8,128)(2,1)}), bf16[176,4096]{1,0:T(8,128)(2,1)}) %all-gather.7.cloned.1.call-update) | async-done | bytes 1441808 | tf_op jit(solution)/shard_map/all_gather | solution.py:139
  276.3 2.1 fusion.32
  278.4 3.1 %fusion.24 = bf16[160,224]{1,0:T(8,128)(2,1)} fusion(f32[160,224]{1,0:T(8,128)S(1)} %fusion.32, bf16[4096,224]{1,0:T(8,128)(2,1)} %reshape.199, bf16[176,4096]{1,0:T(8,128)(2,1)} %all-gather.7.cloned.1.call-done, f32[160]{0:T(256)S(1)} %get-tuple-element.5, f32[224]{0:T(256)S(1)} %convert_element_type.85), kind=kOutput, calls=%fused_computation.22 | convolution fusion | flops 293744640 | bytes 3624448 | tf_op jit(solution)/shard_map/dot_general | solution.py:147
  (36 shorter events, 0.4 us)
Async XLA Ops:
  6.5 17.4 %copy-start = (bf16[64,448,16]{1,2,0:T(8,128)(2,1)S(1)}, bf16[64,448,16]{1,2,0:T(8,128)(2,1)}, u32[]{:S(2)}) copy-start(bf16[64,448,16]{1,2,0:T(8,128)(2,1)} %param.23) | copy-start | bytes 2752516
  6.5 16.6 %copy-start.3 = (s32[16]{0:T(128)S(1)}, s32[16]{0:T(128)}, u32[]{:S(2)}) copy-start(s32[16]{0:T(128)} %param.30) | copy-start | bytes 196
  6.5 16.7 %copy-start.1 = (s32[16]{0:T(128)S(1)}, s32[16]{0:T(128)}, u32[]{:S(2)}) copy-start(s32[16]{0:T(128)} %param.31) | copy-start | bytes 196
  6.5 107.0 %all-gather.9.cloned.1.call-start = ((), (), s32[]{:S(2)}) async-start(), calls=%async_computation.3 | async-start | bytes 2838528 | tf_op jit(solution)/shard_map/all_gather | solution.py:106
  9.0 9.4 %collective-permute-start = (bf16[82,224]{1,0:T(8,128)(2,1)S(1)}, bf16[82,224]{1,0:T(8,128)(2,1)S(1)}, u32[]{:S(2)}, u32[]{:S(2)}) collective-permute-start(bf16[82,224]{1,0:T(8,128)(2,1)S(1)} %get-tuple-element.15), channel_id=1, source_target_pairs={{0,0},{1,1},{2,32},{3,33},{4,64},{5,65},{6,96},{7,97},{8,128},{9,1... | collective-permute-start | bytes 110216 | tf_op jit(solution)/shard_map/ppermute | solution.py:102
  9.7 9.6 %collective-permute-start.1 = (bf16[82,224]{1,0:T(8,128)(2,1)S(1)}, bf16[82,224]{1,0:T(8,128)(2,1)S(1)}, u32[]{:S(2)}, u32[]{:S(2)}) collective-permute-start(bf16[82,224]{1,0:T(8,128)(2,1)S(1)} %get-tuple-element.16), channel_id=1, source_target_pairs={{0,1},{1,0},{2,33},{3,32},{4,65},{5,64},{6,97},{7,96},{8,129},{9,1... | collective-permute-start | bytes 110216 | tf_op jit(solution)/shard_map/ppermute | solution.py:102
  20.0 174.3 %all-gather.5.cloned.1.call-start = ((), (), s32[]{:S(2)}) async-start(), calls=%async_computation.1 | async-start | bytes 7798784 | tf_op jit(solution)/shard_map/all_gather | solution.py:86
  23.2 33.3 %copy-start.2 = (bf16[384]{0:T(512)(128)(2,1)S(1)}, bf16[384]{0:T(512)(128)(2,1)}, u32[]{:S(2)}) copy-start(bf16[384]{0:T(512)(128)(2,1)} %param.20) | copy-start | bytes 2308
  23.2 35.2 %copy-start.4 = (s32[16]{0:T(128)S(1)}, s32[16]{0:T(128)}, u32[]{:S(2)}) copy-start(s32[16]{0:T(128)} %param.29) | copy-start | bytes 196
  23.2 37.2 %copy-start.5 = (s32[16]{0:T(128)S(1)}, s32[16]{0:T(128)}, u32[]{:S(2)}) copy-start(s32[16]{0:T(128)} %param.27) | copy-start | bytes 196
  25.2 41.3 %all-to-all-start = ((bf16[16,448,16]{1,2,0:T(8,128)(2,1)}), bf16[16,448,16]{1,2,0:T(8,128)(2,1)S(1)}, u32[]{:S(2)}, u32[]{:S(2)}) async-start(bf16[16,448,16]{1,2,0:T(8,128)(2,1)} %gather_fusion.1), calls=%async_computation | async-start | bytes 524288 | tf_op jit(solution)/shard_map/all_to_all | solution.py:89
  56.4 219.9 %all-gather.7.cloned.1.call-start = ((), (), s32[]{:S(2)}) async-start(), calls=%async_computation.2 | async-start | bytes 1486848 | tf_op jit(solution)/shard_map/all_gather | solution.py:139
  202.1 2.9 %copy-start.6 = (bf16[224]{0:T(256)(128)(2,1)S(1)}, bf16[224]{0:T(256)(128)(2,1)}, u32[]{:S(2)}) copy-start(bf16[224]{0:T(256)(128)(2,1)} %param.22) | copy-start | bytes 1348
  203.9 1.5 slice-start
Sparse Core Ops, SparseCore 0:
  20.1 93.3 all-gather.8
  116.6 77.6 all-gather.4
  205.1 71.1 all-gather.6

commit v3 on v2

--- a/solution.py
+++ b/solution.py
@@ -6,11 +6,6 @@
 HEAD_SIZE = 128
 GCAP = 160
 WIN = 53
-
-
-def broadcast(x, axis, root):
-    mine = lax.axis_index(axis) == root
-    return lax.psum(jnp.where(mine, x, jnp.zeros_like(x)), axis)
 
 
 def group_layout(prompt, count, suffix):
@@ -50,7 +45,7 @@
     return mixed_rows.astype(jnp.bfloat16).reshape(queries.shape[0], -1)
 
 
-def local(
+def layer(
     hidden,
     ln_gain,
     ln_shift,
@@ -173,4 +168,4 @@
         P(),
     )
     out_specs = P("row", "col")
-    return jax.shard_map(local, mesh=mesh, in_specs=in_specs, out_specs=out_specs, check_vma=False)
+    return jax.shard_map(layer, mesh=mesh, in_specs=in_specs, out_specs=out_specs, check_vma=False)

time: 289 us -> 289 us (level)
  no operation moved by 1% of the time
where the time goes in v3:
time: 289 us; the launch traced here: 288 us
  waiting for transfers between devices  184 us (64%)
  starting transfers between devices  40.7 us (14%)
  local copies, waits for them, and re-layouts  22.5 us (8%)
  between operations  15.4 us (5%)
  matrix products  13.6 us (5%)
  other arithmetic  11.6 us (4%)
    all_gather x1, waiting for transfers between devices, layer(): packed_full = lax.all_gather(packed, 'row', axis=0, tiled=True)  69.7 us
    all_gather x1, waiting for transfers between devices, layer(): lax.all_gather(jnp.concatenate([mixed_rows, down_here], axis=0), 'col', a...  67.7 us
    all_gather x1, waiting for transfers between devices, layer(): gathered = lax.all_gather(mine, 'col', axis=1, tiled=True)  45.9 us
    all_to_all x1, starting transfers between devices, layer(): down_parts = lax.all_to_all(down_qkv[adapters], 'row', 0, 0, tiled=True)  31.2 us
    ppermute x2, starting transfers between devices, layer(): halves.append(lax.ppermute(sent, ('row', 'col'), pairs))  9.41 us
    unnamed x16, local copies, waits for them, and re-layouts  6.34 us
  transfers between devices with their start and end apart: 6, of which 4 were waited for; matrix products, arithmetic and copies ran while one was open for 10% of the time, Pallas kernels for 0%

profile of v3, /device:TPU:1, one launch (start us, length us, event | category | flops | bytes accessed | tf_op | source)
XLA Modules:
  0.0 288.1 jit_solution(9225564456309595381)
XLA Ops:
  6.6 0.8 broadcast_in_dim.42
  7.3 0.7 broadcast_in_dim.43
  8.0 0.9 pad_maximum_fusion.1
  8.9 0.1 constant_dynamic-slice_fusion.2
  9.0 0.7 collective-permute-start
  9.7 8.7 %collective-permute-start.1 = (bf16[82,224]{1,0:T(8,128)(2,1)S(1)}, bf16[82,224]{1,0:T(8,128)(2,1)S(1)}, u32[]{:S(2)}, u32[]{:S(2)}) collective-permute-start(bf16[82,224]{1,0:T(8,128)(2,1)S(1)} %get-tuple-element.16), channel_id=1, source_target_pairs={{0,1},{1,0},{2,33},{3,32},{4,65},{5,64},{6,97},{7,96},{8,129},{9,1... | collective-permute-start | bytes 110216 | tf_op jit(solution)/shard_map/ppermute | solution.py:97
  18.5 0.8 collective-permute-done.1
  19.3 0.6 maximum_bitcast_fusion
  20.0 1.0 copy.27
  21.1 0.3 reshape.195
  21.3 1.8 pad_maximum_fusion
  23.3 0.7 gather_fusion
  23.9 1.3 gather_fusion.1
  25.2 31.2 %all-to-all-start = ((bf16[16,448,16]{1,2,0:T(8,128)(2,1)}), bf16[16,448,16]{1,2,0:T(8,128)(2,1)S(1)}, u32[]{:S(2)}, u32[]{:S(2)}) async-start(bf16[16,448,16]{1,2,0:T(8,128)(2,1)} %gather_fusion.1), calls=%async_computation | async-start | bytes 524288 | tf_op jit(solution)/shard_map/all_to_all | solution.py:84
  56.5 0.6 dynamic_slice.29
  58.4 0.6 dynamic_slice.32
  59.0 1.3 compare_select_fusion.3
  60.4 0.6 dynamic_slice.31
  61.7 0.7 dynamic-slice_bitcast_fusion
  62.4 0.7 add_reduce_fusion
  63.1 0.1 convert_reduce_fusion.1
  63.2 1.3 fusion.56
  64.5 0.1 select_reduce_fusion
  64.6 1.2 fusion.62
  65.9 0.6 broadcast_compare_fusion
  66.5 0.2 copy.28
  66.7 1.0 reshape.196
  67.7 45.9 %all-gather.9.cloned.1.call-done = bf16[32,224,162]{1,2,0:T(8,128)(2,1)} async-done(((bf16[1,224,162]{1,2,0:T(8,128)(2,1)}), bf16[32,224,162]{1,2,0:T(8,128)(2,1)}) %all-gather.9.cloned.1.call-update) | async-done | bytes 2322448 | tf_op jit(solution)/shard_map/all_gather | solution.py:101
  113.6 3.9 %copy.26 = bf16[32,224,162]{1,0,2:T(8,128)(2,1)} copy(bf16[32,224,162]{1,2,0:T(8,128)(2,1)} %all-gather.9.cloned.1.call-done) | data formatting | bytes 4644864 | tf_op jit(solution)/shard_map/all_gather | solution.py:101
  117.5 5.3 %reshape.220 = bf16[7168,162]{0,1:T(8,128)(2,1)S(1)} reshape(bf16[32,224,162]{1,0,2:T(8,128)(2,1)} %copy.26) | data formatting | bytes 4644864
  122.8 0.4 convert_reduce_fusion
  123.2 0.8 fusion.4
  124.0 0.6 add_rsqrt_fusion
  124.6 69.7 %all-gather.5.cloned.1.call-done = bf16[7168,512]{1,0:T(8,128)(2,1)} async-done(((bf16[448,512]{1,0:T(8,128)(2,1)}), bf16[7168,512]{1,0:T(8,128)(2,1)}) %all-gather.5.cloned.1.call-update) | async-done | bytes 7340048 | tf_op jit(solution)/shard_map/all_gather | solution.py:81
  194.3 4.7 %fusion.8 = f32[160,384]{1,0:T(8,128)} fusion(bf16[7168,512]{1,0:T(8,128)(2,1)} %all-gather.5.cloned.1.call-done, f32[384]{0:T(512)S(1)} %convert_element_type.74, f32[7168]{0:T(1024)S(1)} %bitcast.62, f32[7168]{0:T(1024)S(1)} %bitcast.60, f32[160]{0:T(256)} %add_rsqrt_fusion, f32[160]{0:T(256)S(1)} %broadcast_multiply_fusion, ...), kind=kOutput, calls=%fused_computation.13 | convolution fusion | flops 887746560 | bytes 8105984 | tf_op jit(solution)/shard_map/dot_general | solution.py:115
  199.0 3.0 %convolution_add_fusion = f32[160,384]{1,0:T(8,128)} fusion(f32[160,384]{1,0:T(8,128)} %fusion.8, bf16[7168,16]{0,1:T(8,128)(2,1)} %reshape.196, bf16[64,16,384]{2,1,0:T(8,128)(2,1)} %param.24, s32[]{:T(128)S(6)} %select_n.119, f32[7168]{0:T(1024)S(1)} %bitcast.63, f32[7168]{0:T(1024)S(1)} %bitcast.61, f32[160]{0:T(256)} %add_rsqrt_fusion, ...), kind=kOutput, calls=%fused_computation.12 | convolution fusion | flops 45611520 | bytes 3086340 | tf_op jit(solution)/shard_map/dot_general | solution.py:120
  202.1 1.1 reshape.197
  203.2 0.1 fusion.40
  203.3 0.2 fusion.64
  203.4 0.2 fusion.65
  203.7 0.2 fusion.39
  203.9 0.4 fusion.27
  204.3 0.6 pad_maximum_fusion.2
  205.0 0.4 slice-done
  205.4 3.2 %reshape.199 = bf16[4096,224]{1,0:T(8,128)(2,1)} reshape(bf16[7168,128]{1,0:T(8,128)(2,1)S(1)} %slice-done) | data formatting | bytes 3670016 | tf_op jit(solution)/shard_map/reshape | solution.py:83
  208.6 67.7 %all-gather.7.cloned.1.call-done = bf16[176,4096]{1,0:T(8,128)(2,1)} async-done(((bf16[176,128]{1,0:T(8,128)(2,1)}), bf16[176,4096]{1,0:T(8,128)(2,1)}) %all-gather.7.cloned.1.call-update) | async-done | bytes 1441808 | tf_op jit(solution)/shard_map/all_gather | solution.py:134
  276.3 2.1 fusion.32
  278.4 3.1 %fusion.24 = bf16[160,224]{1,0:T(8,128)(2,1)} fusion(f32[160,224]{1,0:T(8,128)S(1)} %fusion.32, bf16[4096,224]{1,0:T(8,128)(2,1)} %reshape.199, bf16[176,4096]{1,0:T(8,128)(2,1)} %all-gather.7.cloned.1.call-done, f32[160]{0:T(256)S(1)} %get-tuple-element.5, f32[224]{0:T(256)S(1)} %convert_element_type.85), kind=kOutput, calls=%fused_computation.22 | convolution fusion | flops 293744640 | bytes 3624448 | tf_op jit(solution)/shard_map/dot_general | solution.py:142
  (36 shorter events, 0.4 us)
Async XLA Ops:
  6.5 17.4 %copy-start = (bf16[64,448,16]{1,2,0:T(8,128)(2,1)S(1)}, bf16[64,448,16]{1,2,0:T(8,128)(2,1)}, u32[]{:S(2)}) copy-start(bf16[64,448,16]{1,2,0:T(8,128)(2,1)} %param.23) | copy-start | bytes 2752516
  6.5 16.6 %copy-start.3 = (s32[16]{0:T(128)S(1)}, s32[16]{0:T(128)}, u32[]{:S(2)}) copy-start(s32[16]{0:T(128)} %param.30) | copy-start | bytes 196
  6.5 16.7 %copy-start.1 = (s32[16]{0:T(128)S(1)}, s32[16]{0:T(128)}, u32[]{:S(2)}) copy-start(s32[16]{0:T(128)} %param.31) | copy-start | bytes 196
  6.5 107.0 %all-gather.9.cloned.1.call-start = ((), (), s32[]{:S(2)}) async-start(), calls=%async_computation.3 | async-start | bytes 2838528 | tf_op jit(solution)/shard_map/all_gather | solution.py:101
  9.0 9.4 %collective-permute-start = (bf16[82,224]{1,0:T(8,128)(2,1)S(1)}, bf16[82,224]{1,0:T(8,128)(2,1)S(1)}, u32[]{:S(2)}, u32[]{:S(2)}) collective-permute-start(bf16[82,224]{1,0:T(8,128)(2,1)S(1)} %get-tuple-element.15), channel_id=1, source_target_pairs={{0,0},{1,1},{2,32},{3,33},{4,64},{5,65},{6,96},{7,97},{8,128},{9,1... | collective-permute-start | bytes 110216 | tf_op jit(solution)/shard_map/ppermute | solution.py:97
  9.7 9.6 %collective-permute-start.1 = (bf16[82,224]{1,0:T(8,128)(2,1)S(1)}, bf16[82,224]{1,0:T(8,128)(2,1)S(1)}, u32[]{:S(2)}, u32[]{:S(2)}) collective-permute-start(bf16[82,224]{1,0:T(8,128)(2,1)S(1)} %get-tuple-element.16), channel_id=1, source_target_pairs={{0,1},{1,0},{2,33},{3,32},{4,65},{5,64},{6,97},{7,96},{8,129},{9,1... | collective-permute-start | bytes 110216 | tf_op jit(solution)/shard_map/ppermute | solution.py:97
  20.0 174.3 %all-gather.5.cloned.1.call-start = ((), (), s32[]{:S(2)}) async-start(), calls=%async_computation.1 | async-start | bytes 7798784 | tf_op jit(solution)/shard_map/all_gather | solution.py:81
  23.2 33.3 %copy-start.2 = (bf16[384]{0:T(512)(128)(2,1)S(1)}, bf16[384]{0:T(512)(128)(2,1)}, u32[]{:S(2)}) copy-start(bf16[384]{0:T(512)(128)(2,1)} %param.20) | copy-start | bytes 2308
  23.2 35.2 %copy-start.4 = (s32[16]{0:T(128)S(1)}, s32[16]{0:T(128)}, u32[]{:S(2)}) copy-start(s32[16]{0:T(128)} %param.29) | copy-start | bytes 196
  23.2 37.2 %copy-start.5 = (s32[16]{0:T(128)S(1)}, s32[16]{0:T(128)}, u32[]{:S(2)}) copy-start(s32[16]{0:T(128)} %param.27) | copy-start | bytes 196
  25.2 41.3 %all-to-all-start = ((bf16[16,448,16]{1,2,0:T(8,128)(2,1)}), bf16[16,448,16]{1,2,0:T(8,128)(2,1)S(1)}, u32[]{:S(2)}, u32[]{:S(2)}) async-start(bf16[16,448,16]{1,2,0:T(8,128)(2,1)} %gather_fusion.1), calls=%async_computation | async-start | bytes 524288 | tf_op jit(solution)/shard_map/all_to_all | solution.py:84
  56.4 219.9 %all-gather.7.cloned.1.call-start = ((), (), s32[]{:S(2)}) async-start(), calls=%async_computation.2 | async-start | bytes 1486848 | tf_op jit(solution)/shard_map/all_gather | solution.py:134
  202.1 2.9 %copy-start.6 = (bf16[224]{0:T(256)(128)(2,1)S(1)}, bf16[224]{0:T(256)(128)(2,1)}, u32[]{:S(2)}) copy-start(bf16[224]{0:T(256)(128)(2,1)} %param.22) | copy-start | bytes 1348
  203.9 1.5 slice-start
Sparse Core Ops, SparseCore 0:
  20.1 93.3 all-gather.8
  116.6 77.6 all-gather.4
  205.1 71.1 all-gather.6

commit v4 on v3

--- a/solution.py
+++ b/solution.py
@@ -98,7 +98,18 @@
     first = jnp.where(parity == 0, halves[0], halves[1])
     second = jnp.where(parity == 0, halves[1], halves[0])
     mine = jnp.concatenate([first[:tokens_here], second], axis=0)
-    gathered = lax.all_gather(mine, "col", axis=1, tiled=True)
+    parity_groups = [list(range(p, col_count, 2)) for p in range(2)]
+    own = lax.all_gather(
+        mine, "col", axis=1, tiled=True, axis_index_groups=parity_groups
+    )
+    other = lax.ppermute(own, "col", [(i, i ^ 1) for i in range(col_count)])
+    even = jnp.where(parity == 0, own, other)
+    odd = jnp.where(parity == 0, other, own)
+    row_count_here = mine.shape[0]
+    gathered = jnp.stack(
+        [even.reshape(row_count_here, -1, chunk), odd.reshape(row_count_here, -1, chunk)],
+        axis=2,
+    ).reshape(row_count_here, -1)
     features = gathered[: 2 * tokens_here]
     gain_full = gathered[2 * tokens_here]
     shift_full = gathered[2 * tokens_here + 1]

time: 289 us -> 289 us (level)
  waiting for transfers between devices: 184 us -> 128 us
  other arithmetic: 11.6 us -> 37.8 us
  local copies, waits for them, and re-layouts: 22.5 us -> 38.9 us
  starting transfers between devices: 40.7 us -> 53.8 us
    all_gather x1, waiting for transfers between devices: 69.7 us -> 14.2 us  [layer(): packed_full = lax.all_gather(packed, 'row', axis=0, tiled=True)]
    ppermute x0 -> x1, starting transfers between devices: none -> 13.1 us  [layer(): other = lax.ppermute(own, 'col', [(i, i ^ 1) for i in range(col_count)])]
    reduce_sum x1, other arithmetic: 0.41 us -> 12.8 us  [layer(): average = jnp.mean(widened, axis=1, keepdims=True)]
    convert_element_type x0 -> x4, local copies, waits for them, and re-layouts: none -> 11.9 us  [the longest x1 6.26 us: layer(): widened = features.astype(jnp.float32)]
    another operation x0 -> x2, local copies, waits for them, and re-layouts: none -> 8.76 us  [layer(): jnp.stack([even.reshape(row_count_here, -1, chunk), odd.reshape(row_count...]
    convert_element_type x0 -> x2, other arithmetic: none -> 6.88 us  [the longest x1 6.02 us: layer(): normed = (centred * lax.rsqrt(spread + 1e-05) * gain_full.astype(jnp.floa...]
    reduce_sum x1, other arithmetic: 0.76 us -> 6.2 us  [layer(): spread = jnp.mean(centred * centred, axis=1, keepdims=True)]
    unnamed x16 -> x18, local copies, waits for them, and re-layouts: 6.34 us -> 4.5 us
  transfers between devices with their start and end apart: 6 -> 7, of which waited for: 4 -> 4; matrix products, arithmetic and copies ran while one was open for 10% -> 25% of each run, Pallas kernels for 0% -> 0%
where the time goes in v4:
time: 289 us; the launch traced here: 288 us
  waiting for transfers between devices  128 us (44%)
  starting transfers between devices  53.8 us (19%)
  local copies, waits for them, and re-layouts  38.9 us (13%)
  other arithmetic  37.8 us (13%)
  between operations  15.4 us (5%)
  matrix products  14.7 us (5%)
    all_gather x1, waiting for transfers between devices, layer(): lax.all_gather(jnp.concatenate([mixed_rows, down_here], axis=0), 'col', a...  67.9 us
    all_gather x1, waiting for transfers between devices, layer(): lax.all_gather(mine, 'col', axis=1, tiled=True, axis_index_groups=parity_...  44.8 us
    all_to_all x1, starting transfers between devices, layer(): down_parts = lax.all_to_all(down_qkv[adapters], 'row', 0, 0, tiled=True)  31.2 us
    all_gather x1, waiting for transfers between devices, layer(): packed_full = lax.all_gather(packed, 'row', axis=0, tiled=True)  14.2 us
    ppermute x1, starting transfers between devices, layer(): other = lax.ppermute(own, 'col', [(i, i ^ 1) for i in range(col_count)])  13.1 us
    reduce_sum x1, other arithmetic, layer(): average = jnp.mean(widened, axis=1, keepdims=True)  12.8 us
    ppermute x2, starting transfers between devices, layer(): halves.append(lax.ppermute(sent, ('row', 'col'), pairs))  9.41 us
    another operation x2, local copies, waits for them, and re-layouts, layer(): jnp.stack([even.reshape(row_count_here, -1, chunk), odd.reshape(row_count...  8.76 us
  transfers between devices with their start and end apart: 7, of which 4 were waited for; matrix products, arithmetic and copies ran while one was open for 25% of the time, Pallas kernels for 0%

profile of v4, /device:TPU:1, one launch (start us, length us, event | category | flops | bytes accessed | tf_op | source)
XLA Modules:
  0.0 288.4 jit_solution(2947161050628913436)
XLA Ops:
  6.6 0.8 broadcast_in_dim.42
  7.3 0.7 broadcast_in_dim.43
  8.0 0.9 pad_maximum_fusion.1
  9.0 0.7 collective-permute-start
  9.7 8.7 %collective-permute-start.1 = (bf16[82,224]{1,0:T(8,128)(2,1)S(1)}, bf16[82,224]{1,0:T(8,128)(2,1)S(1)}, u32[]{:S(2)}, u32[]{:S(2)}) collective-permute-start(bf16[82,224]{1,0:T(8,128)(2,1)S(1)} %get-tuple-element.20), channel_id=1, source_target_pairs={{0,1},{1,0},{2,33},{3,32},{4,65},{5,64},{6,97},{7,96},{8,129},{9,1... | collective-permute-start | bytes 110216 | tf_op jit(solution)/shard_map/ppermute | solution.py:97
  18.5 0.8 collective-permute-done.1
  19.3 0.7 maximum_bitcast_fusion
  20.1 1.0 copy.33
  21.1 0.3 reshape.249
  21.4 1.8 pad_maximum_fusion
  23.2 0.7 gather_fusion
  23.9 1.3 gather_fusion.1
  25.2 31.2 %all-to-all-start = ((bf16[16,448,16]{1,2,0:T(8,128)(2,1)}), bf16[16,448,16]{1,2,0:T(8,128)(2,1)S(1)}, u32[]{:S(2)}, u32[]{:S(2)}) async-start(bf16[16,448,16]{1,2,0:T(8,128)(2,1)} %gather_fusion.1), calls=%async_computation | async-start | bytes 524288 | tf_op jit(solution)/shard_map/all_to_all | solution.py:84
  56.5 0.6 dynamic_slice.32
  57.1 44.8 %all-gather.9.cloned.1.call-done = bf16[16,224,162]{1,2,0:T(8,128)(2,1)} async-done(((bf16[1,224,162]{1,2,0:T(8,128)(2,1)}), bf16[16,224,162]{1,2,0:T(8,128)(2,1)}) %all-gather.9.cloned.1.call-update) | async-done | bytes 1161232 | tf_op jit(solution)/shard_map/all_gather | solution.py:102
  101.9 1.6 copy.30
  103.5 3.5 %reshape.277 = bf16[3584,162]{0,1:T(8,128)(2,1)} reshape(bf16[16,224,162]{1,0,2:T(8,128)(2,1)S(1)} %copy.30) | data formatting | bytes 2322432
  107.0 13.1 %collective-permute-start.2 = (bf16[162,3584]{1,0:T(8,128)(2,1)}, bf16[162,3584]{1,0:T(8,128)(2,1)}, u32[]{:S(2)}, u32[]{:S(2)}) collective-permute-start(bf16[162,3584]{1,0:T(8,128)(2,1)} %bitcast.58), channel_id=1, source_target_pairs={{0,1},{1,0},{2,3},{3,2},{4,5},{5,4},{6,7},{7,6},{8,9},{9,8},{10,11... | collective-permute-start | bytes 3483656 | tf_op jit(solution)/shard_map/ppermute | solution.py:105
  120.1 1.4 compare_select_fusion.3
  121.4 0.6 dynamic_slice.29
  123.5 0.7 dynamic_slice.31
  124.8 0.7 dynamic-slice_bitcast_fusion
  125.5 0.7 add_reduce_fusion
  126.3 1.4 fusion.57
  127.7 1.3 fusion.60
  129.1 0.6 broadcast_compare_fusion
  129.9 1.0 reshape.250
  130.9 1.9 broadcast_select_fusion.1
  132.7 4.4 %stack_reshape.8 = bf16[162,16,1,224]{3,2,1,0:T(2,128)(2,1)} reshape(bf16[162,3584]{1,0:T(8,128)(2,1)S(1)} %get-tuple-element.15) | data formatting | bytes 2322432 | tf_op jit(solution)/shard_map/stack;reshape | solution.py:109
  137.1 4.4 %stack_reshape.9 = bf16[162,16,1,224]{3,2,1,0:T(2,128)(2,1)} reshape(bf16[162,3584]{1,0:T(8,128)(2,1)S(1)} %get-tuple-element.16) | data formatting | bytes 2322432 | tf_op jit(solution)/shard_map/stack;reshape | solution.py:109
  141.5 0.9 fusion.46
  142.6 12.8 %convert_reduce_fusion = (f32[160]{0:T(256)S(1)}, bf16[160,16,2,224]{3,2,1,0:T(2,128)(2,1)}) fusion(bf16[162,16,1,224]{3,2,1,0:T(2,128)(2,1)} %stack_reshape.9, bf16[162,16,1,224]{3,2,1,0:T(2,128)(2,1)} %stack_reshape.8), kind=kLoop, calls=%fused_computation.7 | loop fusion | flops 6881120 | bytes 4616832 | tf_op jit(solution)/shard_map/reduce_sum | solution.py:118
  155.4 6.3 %reshape.254 = f32[160,7168]{1,0:T(8,128)} reshape(bf16[160,16,2,224]{3,2,1,0:T(2,128)(2,1)} %get-tuple-element.12) | data formatting | bytes 6881280 | tf_op jit(solution)/shard_map/convert_element_type | solution.py:117
  161.6 6.2 %multiply_reduce_fusion = f32[160]{0:T(256)S(1)} fusion(bf16[160,16,2,224]{3,2,1,0:T(2,128)(2,1)} %get-tuple-element.12, f32[160]{0:T(256)S(1)} %broadcast_multiply_fusion), kind=kLoop, calls=%fused_computation.5 | loop fusion | flops 4587360 | bytes 2295040 | tf_op jit(solution)/shard_map/reduce_sum | solution.py:120
  167.9 6.0 %add_convert_fusion = bf16[160,16,2,224]{3,2,1,0:T(2,128)(2,1)} fusion(bf16[160,16,2,224]{3,2,1,0:T(2,128)(2,1)S(1)} %copy-done.2, f32[160]{0:T(256)S(1)} %add_rsqrt_fusion, f32[160]{0:T(256)S(1)} %broadcast_multiply_fusion, f32[16,2,224]{2,1,0:T(2,128)S(1)} %bitcast.60, f32[16,2,224]{2,1,0:T(2,128)S(1)} %bitcast.59), kind=kLoop, calls=%fused_computation.4 | loop fusion | flops 6881280 | bytes 4646144 | tf_op jit(solution)/shard_map/convert_element_type | solution.py:124
  173.9 5.5 %convert_element_type.127 = bf16[160,7168]{1,0:T(8,128)(2,1)S(1)} reshape(bf16[160,16,2,224]{3,2,1,0:T(2,128)(2,1)} %add_convert_fusion) | data formatting | bytes 4587520 | tf_op jit(solution)/shard_map/convert_element_type | solution.py:124
  179.4 14.2 %all-gather.5.cloned.1.call-done = bf16[7168,512]{1,0:T(8,128)(2,1)} async-done(((bf16[448,512]{1,0:T(8,128)(2,1)}), bf16[7168,512]{1,0:T(8,128)(2,1)}) %all-gather.5.cloned.1.call-update) | async-done | bytes 7340048 | tf_op jit(solution)/shard_map/all_gather | solution.py:81
  193.5 6.1 %fusion.6 = f32[160,384]{1,0:T(8,128)} fusion(bf16[7168,512]{1,0:T(8,128)(2,1)} %all-gather.5.cloned.1.call-done, f32[160,7168]{1,0:T(8,128)} %reshape.254, f32[7168]{0:T(1024)S(1)} %reshape.256, f32[7168]{0:T(1024)S(1)} %reshape.255, f32[160]{0:T(256)S(1)} %add_rsqrt_fusion, f32[160]{0:T(256)S(1)} %broadcast_multiply_fusion, f32[384]{0:T(512)S(1)} %convert_element_type.121), kind=kOutput, calls=%fused_computation.18 | convolution fusion | flops 886599680 | bytes 10398464 | tf_op jit(solution)/shard_map/dot_general | solution.py:126
  199.6 2.7 convolution_add_fusion
  202.4 1.1 reshape.251
  203.7 0.2 fusion.63
  204.2 0.4 fusion.25
  204.6 0.6 pad_maximum_fusion.2
  205.3 0.2 slice-done
  205.5 3.2 %reshape.253 = bf16[4096,224]{1,0:T(8,128)(2,1)} reshape(bf16[7168,128]{1,0:T(8,128)(2,1)S(1)} %slice-done) | data formatting | bytes 3670016 | tf_op jit(solution)/shard_map/reshape | solution.py:83
  208.7 67.9 %all-gather.7.cloned.1.call-done = bf16[176,4096]{1,0:T(8,128)(2,1)} async-done(((bf16[176,128]{1,0:T(8,128)(2,1)}), bf16[176,4096]{1,0:T(8,128)(2,1)}) %all-gather.7.cloned.1.call-update) | async-done | bytes 1441808 | tf_op jit(solution)/shard_map/all_gather | solution.py:145
  276.6 2.1 fusion.30
  278.7 3.1 %fusion.22 = bf16[160,224]{1,0:T(8,128)(2,1)} fusion(f32[160,224]{1,0:T(8,128)S(1)} %fusion.30, bf16[4096,224]{1,0:T(8,128)(2,1)} %reshape.253, bf16[176,4096]{1,0:T(8,128)(2,1)} %all-gather.7.cloned.1.call-done, f32[160]{0:T(256)S(1)} %get-tuple-element.5, f32[224]{0:T(256)S(1)} %convert_element_type.138), kind=kOutput, calls=%fused_computation.27 | convolution fusion | flops 293744640 | bytes 3624448 | tf_op jit(solution)/shard_map/dot_general | solution.py:153
  (48 shorter events, 1.5 us)
Async XLA Ops:
  6.5 17.4 %copy-start = (bf16[64,448,16]{1,2,0:T(8,128)(2,1)S(1)}, bf16[64,448,16]{1,2,0:T(8,128)(2,1)}, u32[]{:S(2)}) copy-start(bf16[64,448,16]{1,2,0:T(8,128)(2,1)} %param.23) | copy-start | bytes 2752516
  6.5 16.6 %copy-start.4 = (s32[16]{0:T(128)S(1)}, s32[16]{0:T(128)}, u32[]{:S(2)}) copy-start(s32[16]{0:T(128)} %param.30) | copy-start | bytes 196
  6.5 16.7 %copy-start.1 = (s32[16]{0:T(128)S(1)}, s32[16]{0:T(128)}, u32[]{:S(2)}) copy-start(s32[16]{0:T(128)} %param.31) | copy-start | bytes 196
  6.5 95.4 %all-gather.9.cloned.1.call-start = ((), (), s32[]{:S(2)}) async-start(), calls=%async_computation.3 | async-start | bytes 1462272 | tf_op jit(solution)/shard_map/all_gather | solution.py:102
  9.0 9.4 %collective-permute-start = (bf16[82,224]{1,0:T(8,128)(2,1)S(1)}, bf16[82,224]{1,0:T(8,128)(2,1)S(1)}, u32[]{:S(2)}, u32[]{:S(2)}) collective-permute-start(bf16[82,224]{1,0:T(8,128)(2,1)S(1)} %get-tuple-element.19), channel_id=1, source_target_pairs={{0,0},{1,1},{2,32},{3,33},{4,64},{5,65},{6,96},{7,97},{8,128},{9,1... | collective-permute-start | bytes 110216 | tf_op jit(solution)/shard_map/ppermute | solution.py:97
  9.7 9.6 %collective-permute-start.1 = (bf16[82,224]{1,0:T(8,128)(2,1)S(1)}, bf16[82,224]{1,0:T(8,128)(2,1)S(1)}, u32[]{:S(2)}, u32[]{:S(2)}) collective-permute-start(bf16[82,224]{1,0:T(8,128)(2,1)S(1)} %get-tuple-element.20), channel_id=1, source_target_pairs={{0,1},{1,0},{2,33},{3,32},{4,65},{5,64},{6,97},{7,96},{8,129},{9,1... | collective-permute-start | bytes 110216 | tf_op jit(solution)/shard_map/ppermute | solution.py:97
  20.0 173.5 %all-gather.5.cloned.1.call-start = ((), (), s32[]{:S(2)}) async-start(), calls=%async_computation.1 | async-start | bytes 7798784 | tf_op jit(solution)/shard_map/all_gather | solution.py:81
  23.1 33.3 %copy-start.5 = (s32[16]{0:T(128)S(1)}, s32[16]{0:T(128)}, u32[]{:S(2)}) copy-start(s32[16]{0:T(128)} %param.29) | copy-start | bytes 196
  25.2 104.5 %all-to-all-start = ((bf16[16,448,16]{1,2,0:T(8,128)(2,1)}), bf16[16,448,16]{1,2,0:T(8,128)(2,1)S(1)}, u32[]{:S(2)}, u32[]{:S(2)}) async-start(bf16[16,448,16]{1,2,0:T(8,128)(2,1)} %gather_fusion.1), calls=%async_computation | async-start | bytes 524288 | tf_op jit(solution)/shard_map/all_to_all | solution.py:84
  56.4 65.6 %copy-start.3 = (bf16[384]{0:T(512)(128)(2,1)S(1)}, bf16[384]{0:T(512)(128)(2,1)}, u32[]{:S(2)}) copy-start(bf16[384]{0:T(512)(128)(2,1)} %param.20) | copy-start | bytes 2308
  56.4 67.1 %copy-start.6 = (s32[16]{0:T(128)S(1)}, s32[16]{0:T(128)}, u32[]{:S(2)}) copy-start(s32[16]{0:T(128)} %param.27) | copy-start | bytes 196
  56.4 220.2 %all-gather.7.cloned.1.call-start = ((), (), s32[]{:S(2)}) async-start(), calls=%async_computation.2 | async-start | bytes 1486848 | tf_op jit(solution)/shard_map/all_gather | solution.py:145
  107.0 23.9 %collective-permute-start.2 = (bf16[162,3584]{1,0:T(8,128)(2,1)}, bf16[162,3584]{1,0:T(8,128)(2,1)}, u32[]{:S(2)}, u32[]{:S(2)}) collective-permute-start(bf16[162,3584]{1,0:T(8,128)(2,1)} %bitcast.58), channel_id=1, source_target_pairs={{0,1},{1,0},{2,3},{3,2},{4,5},{5,4},{6,7},{7,6},{8,9},{9,8},{10,11... | collective-permute-start | bytes 3483656 | tf_op jit(solution)/shard_map/ppermute | solution.py:105
  161.6 6.2 %copy-start.2 = (bf16[160,16,2,224]{3,2,1,0:T(2,128)(2,1)S(1)}, bf16[160,16,2,224]{3,2,1,0:T(2,128)(2,1)}, u32[]{:S(2)}) copy-start(bf16[160,16,2,224]{3,2,1,0:T(2,128)(2,1)} %get-tuple-element.12) | copy-start | bytes 6881284
  202.4 2.9 copy-start.7
  204.0 1.5 slice-start
Sparse Core Ops, SparseCore 0:
  20.1 81.7 all-gather.8
  105.0 88.5 all-gather.4
  205.4 71.1 all-gather.6
